TPU v7x, 256 devices: a whole 4x4x8 slice. The times are simulated.
256 devices in a mesh: samp: 64 (over x, z, core), blk: 4 (over y).
Axes of the slice: x: 4, y: 4, z: 8, core: 2. Of those that a mesh axis runs over, the one named last changes fastest.
Arguments:
- dosages: bfloat16 [40960, 2048], P('samp', 'blk'), may hold values from 0 to 2
- traits: bfloat16 [16, 40960], P(None, 'samp'), may hold values from -6 to 6
- folds: int32 [40960], P('samp'), may hold values from 0 to 4
Outputs:
- level0: float32 [4, 5, 16, 40960], P(None, None, 'blk', 'samp')
- blend: float32 [16, 40960], P('blk', 'samp')
All inputs are finite; a program needn't handle non-finite values.
Results may differ from a plain program's by a relative error of at most 0.0097.
Values may be sent and summed in bfloat16 or wider, within the bound.
No kernel may reach another device: no remote copies, remote signals or barrier semaphores. Data moves between devices by JAX's collectives and lax.ppermute only.
A program may use at most 64 MiB of HBM per device.

v0:
```python
import jax
import jax.numpy as jnp
from jax import lax
from jax.sharding import PartitionSpec as P

FOLDS = 5
SHRINK = 5


RATIOS = (99.0, 3.0, 1.0, 1.0 / 3.0, 1.0 / 99.0)
EPS = 1e-05
HIGH = lax.Precision.HIGHEST


def solve_batch(systems, right_sides):
    factors = jnp.linalg.cholesky(systems)

    def solve_single(factor, right_side):
        return jax.scipy.linalg.cho_solve((factor, True), right_side)

    return jax.vmap(solve_single)(factors, right_sides)


def shards(dosages, traits, folds):
    rows, width = dosages.shape
    traits_count = traits.shape[0]
    fold_ids = jnp.arange(FOLDS, dtype=jnp.int32)
    masks = (folds[None, :] == fold_ids[:, None]).astype(jnp.float32)
    mask_half = masks.astype(jnp.bfloat16)
    traits_wide = traits.astype(jnp.float32)
    grams = []
    crosses = []
    for fold in range(FOLDS):
        weighted = dosages * mask_half[fold][:, None]
        grams.append(jnp.einsum("ri,rj->ij", dosages, weighted, preferred_element_type=jnp.float32))
        crosses.append(
            jnp.dot(traits * mask_half[fold][None, :], dosages, preferred_element_type=jnp.float32)
        )
    gram = jnp.stack(grams)
    cross = jnp.stack(crosses)
    sums = jnp.dot(mask_half, dosages, preferred_element_type=jnp.float32)
    counts = jnp.sum(masks, axis=1)
    trait_sums = jnp.einsum("ks,ts->kt", masks, traits_wide, precision=HIGH)
    gram, sums, cross, counts, trait_sums = lax.psum(
        (gram, sums, cross, counts, trait_sums), "samp"
    )
    total = jnp.sum(counts)
    mean = jnp.sum(sums, axis=0) / total
    gram_total = jnp.sum(gram, axis=0)
    variance = jnp.diagonal(gram_total) / total - mean * mean
    scale = lax.rsqrt(variance + EPS)
    sums_total = jnp.sum(sums, axis=0)
    cross_total = jnp.sum(cross, axis=0)
    trait_total = jnp.sum(trait_sums, axis=0)
    ratios = jnp.array(RATIOS, dtype=jnp.float32)
    identity = jnp.eye(width, dtype=jnp.float32)

    def train_system(fold):
        train_gram = gram_total - lax.dynamic_index_in_dim(gram, fold, 0, keepdims=False)
        train_sums = sums_total - lax.dynamic_index_in_dim(sums, fold, 0, keepdims=False)
        train_count = total - lax.dynamic_index_in_dim(counts, fold, 0, keepdims=False)
        train_cross = cross_total - lax.dynamic_index_in_dim(cross, fold, 0, keepdims=False)
        train_traits = trait_total - lax.dynamic_index_in_dim(trait_sums, fold, 0, keepdims=False)
        centered = (
            train_gram
            - mean[:, None] * train_sums[None, :]
            - train_sums[:, None] * mean[None, :]
            + train_count * mean[:, None] * mean[None, :]
        )
        system = scale[:, None] * centered * scale[None, :]
        target = scale[:, None] * (train_cross.T - mean[:, None] * train_traits[None, :])
        return (system, target)

    systems_count = FOLDS * SHRINK
    per_device = -(-systems_count // lax.axis_size("samp"))
    first = lax.axis_index("samp") * per_device

    def solve_own(offset):
        which = jnp.minimum(first + offset, systems_count - 1)
        fold = which // SHRINK
        shrink = which - fold * SHRINK
        system, target = train_system(fold)
        penalty = jnp.sum(
            jnp.where(jnp.arange(SHRINK, dtype=jnp.int32) == shrink, ratios * width, 0.0)
        )
        beta = solve_batch((system + penalty * identity)[None], target[None])[0]
        return (scale[:, None] * beta).astype(jnp.bfloat16)

    owned = lax.map(solve_own, jnp.arange(per_device, dtype=jnp.int32))
    collected = lax.all_gather(owned, "samp", axis=0, tiled=True)
    coef = collected[:systems_count].reshape(FOLDS, SHRINK, width, traits_count)
    coef_flat = coef.transpose(2, 0, 1, 3).reshape(width, FOLDS * SHRINK * traits_count)
    shift = jnp.einsum("v,klvt->klt", mean, coef.astype(jnp.float32), precision=HIGH)
    raw = jnp.einsum("vc,rv->cr", coef_flat, dosages, preferred_element_type=jnp.float32)
    outcome = raw.reshape(FOLDS, SHRINK, traits_count, rows) - shift[..., None]
    level_pred = jnp.einsum("kltr,kr->ltr", outcome, masks, precision=HIGH)
    group = traits_count // lax.axis_size("blk")
    start = lax.axis_index("blk") * group
    own_traits = lax.dynamic_slice_in_dim(traits_wide, start, group, 0)
    moment_sum, moment_sq = lax.psum(
        (jnp.sum(level_pred, axis=-1), jnp.sum(level_pred * level_pred, axis=-1)), "samp"
    )
    pred_mean = moment_sum / total
    pred_var = moment_sq / total - pred_mean * pred_mean
    moved = (level_pred - pred_mean[..., None]) * lax.rsqrt(pred_var + EPS)[..., None]
    arrived = lax.all_to_all(moved[None], "blk", split_axis=2, concat_axis=0, tiled=True)
    count_pred = arrived.shape[0] * arrived.shape[1]
    flat = arrived.reshape(count_pred, group, rows)
    fold_grams = jnp.einsum("ks,ats,bts->ktab", masks, flat, flat, precision=HIGH)
    fold_cross = jnp.einsum("ks,ats,ts->kta", masks, flat, own_traits, precision=HIGH)
    fold_grams, fold_cross = lax.psum((fold_grams, fold_cross), "samp")
    level0 = flat.reshape(arrived.shape)
    train_grams = jnp.sum(fold_grams, axis=0)[None] - fold_grams
    train_cross = jnp.sum(fold_cross, axis=0)[None] - fold_cross
    shrunk = train_grams + total / 4.0 * jnp.eye(count_pred, dtype=jnp.float32)
    weights = solve_batch(
        shrunk.reshape(-1, count_pred, count_pred), train_cross.reshape(-1, count_pred)
    )
    weights = weights.reshape(FOLDS, group, count_pred)
    every_fold = jnp.einsum("ats,kta->kts", flat, weights, precision=HIGH)
    blended = jnp.einsum("kts,ks->ts", every_fold, masks, precision=HIGH)
    blend_sum, blend_sq = lax.psum(
        (jnp.sum(blended, axis=-1), jnp.sum(blended * blended, axis=-1)), "samp"
    )
    blend_mean = blend_sum / total
    blend_var = blend_sq / total - blend_mean * blend_mean
    blend = (blended - blend_mean[:, None]) * lax.rsqrt(blend_var + EPS)[:, None]
    return (level0, blend)


def solution(mesh):
    in_specs = (P("samp", "blk"), P(None, "samp"), P("samp"))
    out_specs = (P(None, None, "blk", "samp"), P("blk", "samp"))
    return jax.shard_map(shards, mesh=mesh, in_specs=in_specs, out_specs=out_specs, check_vma=False)
```

profile of v0, /device:TPU:8, one launch (start us, length us, event | category | flops | bytes accessed | tf_op | source)
XLA Modules:
  0.0 1097.7 jit_solution(9628487864287836600)
XLA Ops:
  7.2 0.8 convert_bitcast_fusion
  8.0 3.0 fusion.4
  11.0 1.3 fusion.25
  12.3 3.0 fusion.3
  15.5 1.7 fusion.2
  17.4 1.8 fusion.1
  19.3 1.7 fusion
  21.2 0.7 copy-done.5
  22.5 254.1 %all-reduce.4 = (f32[5,512]{1,0:T(8,128)S(1)}, f32[5]{0:T(128)S(1)}, f32[5,16]{1,0:T(8,128)S(1)}) all-reduce(f32[5,512]{1,0:T(8,128)S(1)} %fusion.107, f32[5]{0:T(128)S(1)} %convert_reduce_fusion, f32[5,16]{1,0:T(8,128)S(1)} %fusion.91), channel_id=1, replica_groups=mesh['samp'=64,'blk'=4] {'samp'}, use_global_device_ids=true, to_apply=%region_5.0 | all-reduce | flops 2645 | bytes 21160 | tf_op jit(solution)/shard_map/psum | solution.py:44
  279.0 0.6 fusion.108
  280.2 3.3 reduce_sum.128
  283.5 5.0 gather_fusion
  289.1 2.3 fusion.38
  292.0 1.0 copy-done.2
  293.0 11.7 %custom-call.57 = f32[1,128,128]{2,1,0:T(8,128)S(1)} custom-call(f32[1,128,128]{2,1,0:T(8,128)S(1)} %cholesky.302), custom_call_target="Cholesky" | custom-call | tf_op jit(solution)/shard_map/while/body/eval_jaxpr/jit(cholesky)/cholesky | solution.py:16
  304.9 9.8 custom-call.58
  314.7 1.2 fusion.64
  316.0 1.2 fusion.14
  317.3 11.7 %custom-call.59 = f32[1,128,128]{2,1,0:T(8,128)S(1)} custom-call(f32[1,128,128]{2,1,0:T(8,128)S(1)} %cholesky.306), custom_call_target="Cholesky" | custom-call | tf_op jit(solution)/shard_map/while/body/eval_jaxpr/jit(cholesky)/cholesky | solution.py:16
  329.3 10.0 custom-call.60
  339.6 1.5 fusion.16
  341.1 11.7 %custom-call.61 = f32[1,128,128]{2,1,0:T(8,128)S(1)} custom-call(f32[1,128,128]{2,1,0:T(8,128)S(1)} %cholesky.311), custom_call_target="Cholesky" | custom-call | tf_op jit(solution)/shard_map/while/body/eval_jaxpr/jit(cholesky)/cholesky | solution.py:16
  353.0 9.8 custom-call.62
  363.1 1.3 fusion.19
  364.4 11.9 %custom-call.63 = f32[1,128,128]{2,1,0:T(8,128)S(1)} custom-call(f32[1,128,128]{2,1,0:T(8,128)S(1)} %fusion.19), custom_call_target="Cholesky" | custom-call | tf_op jit(solution)/shard_map/while/body/eval_jaxpr/jit(cholesky)/cholesky | solution.py:16
  376.5 0.7 compare_reduce_fusion.2
  377.2 0.6 compare_reduce_fusion.1
  377.8 0.7 compare_reduce_fusion.3
  381.2 8.9 while.1
  381.9 1.4 constant_dynamic-slice_fusion.8
  384.1 1.4 constant_dynamic-slice_fusion.8
  386.3 1.4 constant_dynamic-slice_fusion.8
  388.6 1.4 constant_dynamic-slice_fusion.8
  390.1 39.3 %custom-call.64 = f32[1,4,128,128]{2,3,1,0:T(8,128)S(1)} custom-call(f32[1,4,128,128]{3,2,1,0:T(8,128)S(1)} %bitcast.390), custom_call_target="InvertDiagBlocksLowerTriangular" | custom-call | tf_op jit(solution)/shard_map/while/body/eval_jaxpr/vmap(jit(_cho_solve))/triangular_solve | solution.py:19
  432.5 0.7 fusion.73
  433.2 70.8 %all-gather.2.cloned.1.call-done = bf16[64,512,16]{1,2,0:T(8,128)(2,1)} async-done(((bf16[1,512,16]{1,2,0:T(8,128)(2,1)}), bf16[64,512,16]{1,2,0:T(8,128)(2,1)}) %all-gather.2.cloned.1.call-update) | async-done | bytes 1048592 | tf_op jit(solution)/shard_map/all_gather | solution.py:90
  504.1 1.0 slice.254
  505.1 1.5 fusion.118
  507.2 128.6 %all-reduce.3 = (f32[5,16]{1,0:T(8,128)S(1)}, f32[5,16]{1,0:T(8,128)S(1)}) all-reduce(f32[5,16]{1,0:T(8,128)S(1)} %get-tuple-element.90, f32[5,16]{1,0:T(8,128)S(1)} %get-tuple-element.89), channel_id=1, replica_groups=mesh['samp'=64,'blk'=4] {'samp'}, use_global_device_ids=true, to_apply=%region_23.24 | all-reduce | flops 160 | bytes 1280 | tf_op jit(solution)/shard_map/psum | solution.py:100
  636.5 0.9 copy.84
  637.4 4.8 all-to-all-start
  642.8 4.3 all-to-all-done
  647.8 1.4 fusion.11
  649.2 246.3 %all-reduce.2 = (f32[5,4,20,20]{3,2,0,1:T(8,128)S(1)}, f32[5,4,20]{2,0,1:T(8,128)S(1)}) all-reduce(f32[5,4,20,20]{3,2,0,1:T(8,128)S(1)} %fusion.11, f32[5,4,20]{2,0,1:T(8,128)S(1)} %fusion.59), channel_id=1, replica_groups=mesh['samp'=64,'blk'=4] {'samp'}, use_global_device_ids=true, to_apply=%region_24.25 | all-reduce | flops 8400 | bytes 67200 | tf_op jit(solution)/shard_map/psum | solution.py:111
  896.0 36.7 %custom-call.65 = f32[20,20,20]{2,1,0:T(8,128)S(1)} custom-call(f32[20,20,20]{2,1,0:T(8,128)S(1)} %fusion.52), custom_call_target="Cholesky" | custom-call | tf_op jit(solution)/shard_map/jit(cholesky)/cholesky | solution.py:16
  933.0 30.9 %custom-call.66 = f32[20,1,20,20]{2,3,1,0:T(8,128)S(1)} custom-call(f32[20,1,20,20]{3,2,1,0:T(8,128)S(1)} %select_bitcast_fusion), custom_call_target="InvertDiagBlocksLowerTriangular" | custom-call | tf_op jit(solution)/shard_map/vmap(jit(_cho_solve))/triangular_solve | solution.py:19
  965.3 124.1 %all-reduce.1 = (f32[4]{0:T(128)S(1)}, f32[4]{0:T(128)S(1)}) all-reduce(f32[4]{0:T(128)S(1)} %get-tuple-element.92, f32[4]{0:T(128)S(1)} %get-tuple-element.91), channel_id=1, replica_groups=mesh['samp'=64,'blk'=4] {'samp'}, use_global_device_ids=true, to_apply=%region_31.32 | all-reduce | flops 8 | bytes 64 | tf_op jit(solution)/shard_map/psum | solution.py:122
  1090.0 0.7 multiply_bitcast_fusion.1
  (126 shorter events, 16.8 us)
Async XLA Ops:
  7.2 8.1 copy-start
  7.2 8.1 copy-start.3
  7.2 273.0 %all-reduce.8.cloned.1.call-start = ((), (), s32[]{:S(2)}) async-start(), calls=%async_computation.2 | async-start | bytes 10813440 | tf_op jit(solution)/shard_map/psum | solution.py:44
  19.1 2.9 copy-start.6
  19.1 259.8 %copy-start.7 = (f32[5]{0:T(128)S(1)}, f32[5]{0:T(128)}, u32[]{:S(2)}) copy-start(f32[5]{0:T(128)} %constant.327) | copy-start | bytes 64
  21.2 0.7 copy-start.5
  21.9 482.2 %all-gather.2.cloned.1.call-start = ((), (), s32[]{:S(2)}) async-start(), calls=%async_computation.1 | async-start | bytes 1064960 | tf_op jit(solution)/shard_map/all_gather | solution.py:90
  292.0 1.0 copy-start.2
  293.0 136.5 %copy-start.4 = (f32[5,16,512]{2,1,0:T(8,128)S(1)}, f32[5,16,512]{2,1,0:T(8,128)}, u32[]{:S(2)}) copy-start(f32[5,16,512]{2,1,0:T(8,128)} %get-tuple-element.116) | copy-start | bytes 491524
  637.4 9.7 all-to-all-start
  647.2 443.4 %copy-start.1 = (f32[4,1,5,4,640]{4,3,2,0,1:T(4,128)}, f32[4,1,5,4,640]{4,3,2,0,1:T(4,128)S(1)}, u32[]{:S(2)}) copy-start(f32[4,1,5,4,640]{4,3,2,0,1:T(4,128)S(1)} %copy.142) | copy-start | bytes 614404
Sparse Core Ops, SparseCore 0:
  22.0 201.9 all-reduce.7
  433.3 70.7 all-gather.1
where the time goes:
time: 1100 us
  blocking collectives  753 us (68%)
  other arithmetic  198 us (18%)
  waiting for transfers between devices  75.2 us (7%)
  matrix products  27.3 us (2%)
  local copies, waits for them, and re-layouts  19.7 us (2%)
  between operations  19.1 us (2%)
    psum x1, blocking collectives, shards(): lax.psum((gram, sums, cross, counts, trait_sums), 'samp')  254 us
    psum x1, blocking collectives, shards(): fold_grams, fold_cross = lax.psum((fold_grams, fold_cross), 'samp')  246 us
    psum x1, blocking collectives, shards(): lax.psum((jnp.sum(level_pred, axis=-1), jnp.sum(level_pred * level_pred,...  129 us
    psum x1, blocking collectives, shards(): lax.psum((jnp.sum(blended, axis=-1), jnp.sum(blended * blended, axis=-1))...  124 us
    another operation x18, other arithmetic, solve_batch(): factors = jnp.linalg.cholesky(systems)  116 us
    all_gather x1, waiting for transfers between devices, shards(): collected = lax.all_gather(owned, 'samp', axis=0, tiled=True)  70.8 us
    another operation x6, other arithmetic, solve_single(): return jax.scipy.linalg.cho_solve((factor, True), right_side)  70.5 us
  transfers between devices with their start and end apart: 3, of which 2 were waited for; matrix products, arithmetic and copies ran while one was open for 0% of the time, Pallas kernels for 0%

commit v1 on v0

v1 whole, which is shorter than its diff:
```python
import jax
import jax.numpy as jnp
import numpy as np
from jax import lax
from jax.sharding import Mesh
from jax.sharding import PartitionSpec as P

FOLDS = 5
SHRINK = 5


RATIOS = (99.0, 3.0, 1.0, 1.0 / 3.0, 1.0 / 99.0)
EPS = 1e-05
HIGH = lax.Precision.HIGHEST
SAMP = ("x", "z", "c")


def solve_batch(systems, right_sides):
    factors = jnp.linalg.cholesky(systems)

    def solve_single(factor, right_side):
        return jax.scipy.linalg.cho_solve((factor, True), right_side)

    return jax.vmap(solve_single)(factors, right_sides)


def psum_tree(value):
    for name in ("c", "z", "x"):
        value = lax.psum(value, name)
    return value


def shards(dosages, traits, folds):
    rows, width = dosages.shape
    traits_count = traits.shape[0]
    fold_ids = jnp.arange(FOLDS, dtype=jnp.int32)
    masks = (folds[None, :] == fold_ids[:, None]).astype(jnp.float32)
    mask_half = masks.astype(jnp.bfloat16)
    traits_wide = traits.astype(jnp.float32)
    augmented = jnp.concatenate(
        [dosages, jnp.ones((rows, 1), jnp.bfloat16), traits.T], axis=1
    )
    weighted = mask_half[:, :, None] * augmented[None]
    stats = jnp.einsum("ri,krj->kij", augmented, weighted, preferred_element_type=jnp.float32)
    stats = lax.psum(stats, SAMP)
    gram = stats[:, :width, :width]
    sums = stats[:, :width, width]
    counts = stats[:, width, width]
    cross = stats[:, width + 1 :, :width]
    trait_sums = stats[:, width + 1 :, width]
    total = jnp.sum(counts)
    mean = jnp.sum(sums, axis=0) / total
    gram_total = jnp.sum(gram, axis=0)
    variance = jnp.diagonal(gram_total) / total - mean * mean
    scale = lax.rsqrt(variance + EPS)
    sums_total = jnp.sum(sums, axis=0)
    cross_total = jnp.sum(cross, axis=0)
    trait_total = jnp.sum(trait_sums, axis=0)
    ratios = jnp.array(RATIOS, dtype=jnp.float32)
    identity = jnp.eye(width, dtype=jnp.float32)

    def train_system(fold):
        train_gram = gram_total - lax.dynamic_index_in_dim(gram, fold, 0, keepdims=False)
        train_sums = sums_total - lax.dynamic_index_in_dim(sums, fold, 0, keepdims=False)
        train_count = total - lax.dynamic_index_in_dim(counts, fold, 0, keepdims=False)
        train_cross = cross_total - lax.dynamic_index_in_dim(cross, fold, 0, keepdims=False)
        train_traits = trait_total - lax.dynamic_index_in_dim(trait_sums, fold, 0, keepdims=False)
        centered = (
            train_gram
            - mean[:, None] * train_sums[None, :]
            - train_sums[:, None] * mean[None, :]
            + train_count * mean[:, None] * mean[None, :]
        )
        system = scale[:, None] * centered * scale[None, :]
        target = scale[:, None] * (train_cross.T - mean[:, None] * train_traits[None, :])
        return (system, target)

    systems_count = FOLDS * SHRINK
    samp_size = lax.axis_size(SAMP)
    per_device = -(-systems_count // samp_size)
    first = lax.axis_index(SAMP) * per_device

    def solve_own(offset):
        which = jnp.minimum(first + offset, systems_count - 1)
        fold = which // SHRINK
        shrink = which - fold * SHRINK
        system, target = train_system(fold)
        penalty = jnp.sum(
            jnp.where(jnp.arange(SHRINK, dtype=jnp.int32) == shrink, ratios * width, 0.0)
        )
        beta = solve_batch((system + penalty * identity)[None], target[None])[0]
        return (scale[:, None] * beta).astype(jnp.bfloat16)

    owned = lax.map(solve_own, jnp.arange(per_device, dtype=jnp.int32))
    collected = lax.all_gather(owned, SAMP, axis=0, tiled=True)
    coef = collected[:systems_count].reshape(FOLDS, SHRINK, width, traits_count)
    coef_flat = coef.transpose(2, 0, 1, 3).reshape(width, FOLDS * SHRINK * traits_count)
    shift = jnp.einsum("v,klvt->klt", mean, coef.astype(jnp.float32), precision=HIGH)
    raw = jnp.einsum("vc,rv->cr", coef_flat, dosages, preferred_element_type=jnp.float32)
    outcome = raw.reshape(FOLDS, SHRINK, traits_count, rows) - shift[..., None]
    level_pred = jnp.einsum("kltr,kr->ltr", outcome, masks, precision=HIGH)
    group = traits_count // lax.axis_size("blk")
    start = lax.axis_index("blk") * group
    own_traits = lax.dynamic_slice_in_dim(traits_wide, start, group, 0)
    own_sums = lax.dynamic_slice_in_dim(trait_sums, start, group, 1)
    arrived = lax.all_to_all(level_pred[None], "blk", split_axis=2, concat_axis=0, tiled=True)
    count_pred = arrived.shape[0] * arrived.shape[1]
    flat = arrived.reshape(count_pred, group, rows)
    raw_grams = jnp.einsum("ks,ats,bts->ktab", masks, flat, flat, precision=HIGH)
    raw_sums = jnp.einsum("ks,ats->kta", masks, flat, precision=HIGH)
    raw_cross = jnp.einsum("ks,ats,ts->kta", masks, flat, own_traits, precision=HIGH)
    packed = jnp.concatenate(
        [raw_grams.reshape(FOLDS * group, count_pred * count_pred),
         raw_sums.reshape(FOLDS * group, count_pred),
         raw_cross.reshape(FOLDS * group, count_pred)],
        axis=1,
    )
    packed = psum_tree(packed)
    raw_grams = packed[:, : count_pred * count_pred].reshape(FOLDS, group, count_pred, count_pred)
    raw_sums = packed[:, count_pred * count_pred : count_pred * (count_pred + 1)].reshape(
        FOLDS, group, count_pred
    )
    raw_cross = packed[:, count_pred * (count_pred + 1) :].reshape(FOLDS, group, count_pred)
    pred_sum = jnp.sum(raw_sums, axis=0)
    pred_sq = jnp.sum(jnp.diagonal(raw_grams, axis1=2, axis2=3), axis=0)
    pred_mean = pred_sum / total
    pred_var = pred_sq / total - pred_mean * pred_mean
    pred_scale = lax.rsqrt(pred_var + EPS)
    level0 = (flat - pred_mean.T[:, :, None]) * pred_scale.T[:, :, None]
    fold_mean = pred_mean[None]
    fold_sums = (raw_sums - counts[:, None, None] * fold_mean) * pred_scale[None]
    fold_grams = (
        raw_grams
        - fold_mean[..., :, None] * raw_sums[..., None, :]
        - raw_sums[..., :, None] * fold_mean[..., None, :]
        + counts[:, None, None, None] * fold_mean[..., :, None] * fold_mean[..., None, :]
    ) * (pred_scale[None, :, :, None] * pred_scale[None, :, None, :])
    fold_cross = (raw_cross - fold_mean * own_sums[:, :, None]) * pred_scale[None]
    level0 = level0.reshape(arrived.shape)
    train_grams = jnp.sum(fold_grams, axis=0)[None] - fold_grams
    train_cross = jnp.sum(fold_cross, axis=0)[None] - fold_cross
    shrunk = train_grams + total / 4.0 * jnp.eye(count_pred, dtype=jnp.float32)
    weights = solve_batch(
        shrunk.reshape(-1, count_pred, count_pred), train_cross.reshape(-1, count_pred)
    )
    weights = weights.reshape(FOLDS, group, count_pred)
    every_fold = jnp.einsum("ats,kta->kts", level0.reshape(flat.shape), weights, precision=HIGH)
    blended = jnp.einsum("kts,ks->ts", every_fold, masks, precision=HIGH)
    blend_sum = jnp.einsum("kta,kta->t", weights, fold_sums, precision=HIGH)
    blend_sq = jnp.einsum("kta,ktab,ktb->t", weights, fold_grams, weights, precision=HIGH)
    blend_mean = blend_sum / total
    blend_var = blend_sq / total - blend_mean * blend_mean
    blend = (blended - blend_mean[:, None]) * lax.rsqrt(blend_var + EPS)[:, None]
    return (level0, blend)


def view_of(mesh):
    devices = np.asarray(mesh.devices)
    samp, blk = devices.shape
    flat = list(devices.reshape(-1))
    xs = sorted({d.coords[0] for d in flat})
    zs = sorted({d.coords[2] for d in flat})
    cores = samp // (len(xs) * len(zs))
    view = devices.reshape(len(xs), len(zs), cores, blk)
    for (i, j, c, b), d in np.ndenumerate(view):
        assert d.coords[0] == xs[i] and d.coords[2] == zs[j]
    return Mesh(view, ("x", "z", "c", "blk"))


def solution(mesh):
    view = view_of(mesh)
    in_specs = (P(SAMP, "blk"), P(None, SAMP), P(SAMP))
    out_specs = (P(None, None, "blk", SAMP), P("blk", SAMP))
    return jax.shard_map(shards, mesh=view, in_specs=in_specs, out_specs=out_specs, check_vma=False)
```

time: 1100 us -> 611 us (0.56)
  blocking collectives: 753 us -> 48.9 us
  waiting for transfers between devices: 75.2 us -> 283 us
  other arithmetic: 198 us -> 210 us
    psum x4 -> x3, blocking collectives: 753 us -> 48.9 us  [psum_tree(): value = lax.psum(value, name)]
    psum x1, waiting for transfers between devices: 0.02 us -> 204 us  [shards(): stats = lax.psum(stats, SAMP)]
    slice x0 -> x5, other arithmetic: none -> 11.1 us  [the longest x1 6.1 us: shards(): gram = stats[:, :width, :width]]
  transfers between devices with their start and end apart: 3 -> 3, of which waited for: 2 -> 3; matrix products, arithmetic and copies ran while one was open for 0% -> 0% of each run, Pallas kernels for 0% -> 0%
where the time goes in v1:
time: 611 us; the launch traced here: 606 us
  waiting for transfers between devices  283 us (46%)
  other arithmetic  210 us (34%)
  blocking collectives  48.9 us (8%)
  local copies, waits for them, and re-layouts  23.7 us (4%)
  between operations  19.3 us (3%)
  matrix products  16.7 us (3%)
    psum x1, waiting for transfers between devices, shards(): stats = lax.psum(stats, SAMP)  204 us
    another operation x18, other arithmetic, solve_batch(): factors = jnp.linalg.cholesky(systems)  116 us
    all_gather x1, waiting for transfers between devices, shards(): collected = lax.all_gather(owned, SAMP, axis=0, tiled=True)  74.5 us
    another operation x6, other arithmetic, solve_single(): return jax.scipy.linalg.cho_solve((factor, True), right_side)  70.5 us
    psum x3, blocking collectives, psum_tree(): value = lax.psum(value, name)  48.9 us
  transfers between devices with their start and end apart: 3, of which 3 were waited for; matrix products, arithmetic and copies ran while one was open for 0% of the time, Pallas kernels for 0%

profile of v1, /device:TPU:8, one launch (start us, length us, event | category | flops | bytes accessed | tf_op | source)
XLA Modules:
  0.0 606.5 jit_solution(15835812869913055414)
XLA Ops:
  7.2 1.4 copy.176
  8.6 1.3 convert_bitcast_fusion
  9.9 0.9 pad_maximum_fusion
  10.8 5.5 fusion.2
  17.6 203.8 %all-reduce.3.cloned.1.call-done = f32[5,529,529]{1,2,0:T(8,128)} async-done(((f32[5,529,529]{1,2,0:T(8,128)}), f32[5,529,529]{1,2,0:T(8,128)}) %all-reduce.3.cloned.1.call-update) | async-done | bytes 5596836 | tf_op jit(solution)/shard_map/psum | solution.py:45
  221.4 1.5 slice_reduce_fusion.1
  223.4 0.9 fusion.108
  225.5 6.1 %fusion.109 = (f32[5,512,512]{1,2,0:T(8,128)}, f32[512,512]{0,1:T(8,128)S(1)}) fusion(f32[5,529,529]{1,2,0:T(8,128)} %all-reduce.3.cloned.1.call-done), kind=kLoop, calls=%fused_computation.227 | loop fusion | flops 1048576 | bytes 11534336 | tf_op jit(solution)/shard_map/slice | solution.py:46
  231.6 4.7 gather_fusion
  237.5 2.4 fusion.35
  240.5 11.7 %custom-call.57 = f32[1,128,128]{2,1,0:T(8,128)S(1)} custom-call(f32[1,128,128]{2,1,0:T(8,128)S(1)} %cholesky.302), custom_call_target="Cholesky" | custom-call | tf_op jit(solution)/shard_map/while/body/eval_jaxpr/jit(cholesky)/cholesky | solution.py:19
  252.3 9.8 %custom-call.58 = f32[1,1,128,128]{2,3,1,0:T(8,128)S(1)} custom-call(f32[1,1,128,128]{3,2,1,0:T(8,128)S(1)} %get-tuple-element.131), custom_call_target="InvertDiagBlocksLowerTriangular" | custom-call | tf_op jit(solution)/shard_map/while/body/eval_jaxpr/jit(cholesky)/cholesky | solution.py:19
  263.0 11.7 %custom-call.59 = f32[1,128,128]{2,1,0:T(8,128)S(1)} custom-call(f32[1,128,128]{2,1,0:T(8,128)S(1)} %cholesky.306), custom_call_target="Cholesky" | custom-call | tf_op jit(solution)/shard_map/while/body/eval_jaxpr/jit(cholesky)/cholesky | solution.py:19
  275.0 10.0 %custom-call.60 = f32[1,1,128,128]{2,3,1,0:T(8,128)S(1)} custom-call(f32[1,1,128,128]{3,2,1,0:T(8,128)S(1)} %get-tuple-element.129), custom_call_target="InvertDiagBlocksLowerTriangular" | custom-call | tf_op jit(solution)/shard_map/while/body/eval_jaxpr/jit(cholesky)/cholesky | solution.py:19
  285.9 11.7 %custom-call.61 = f32[1,128,128]{2,1,0:T(8,128)S(1)} custom-call(f32[1,128,128]{2,1,0:T(8,128)S(1)} %cholesky.311), custom_call_target="Cholesky" | custom-call | tf_op jit(solution)/shard_map/while/body/eval_jaxpr/jit(cholesky)/cholesky | solution.py:19
  297.8 9.8 %custom-call.62 = f32[1,1,128,128]{2,3,1,0:T(8,128)S(1)} custom-call(f32[1,1,128,128]{3,2,1,0:T(8,128)S(1)} %get-tuple-element.127), custom_call_target="InvertDiagBlocksLowerTriangular" | custom-call | tf_op jit(solution)/shard_map/while/body/eval_jaxpr/jit(cholesky)/cholesky | solution.py:19
  308.4 12.1 %custom-call.63 = f32[1,128,128]{2,1,0:T(8,128)S(1)} custom-call(f32[1,128,128]{2,1,0:T(8,128)S(1)} %fusion.21), custom_call_target="Cholesky" | custom-call | tf_op jit(solution)/shard_map/while/body/eval_jaxpr/jit(cholesky)/cholesky | solution.py:19
  320.6 0.6 compare_reduce_fusion.2
  321.3 0.7 compare_reduce_fusion.1
  321.9 0.7 compare_reduce_fusion.3
  325.3 8.1 %while.1 = (s32[]{:T(128)}, f32[1,512,512]{1,2,0:T(8,128)S(1)}, s32[4,2]{0,1:T(2,128)S(1)}, f32[4,1,128,128]{3,2,1,0:T(8,128)S(1)}, s32[]{:T(128)}) while((s32[]{:T(128)}, f32[1,512,512]{1,2,0:T(8,128)S(1)}, s32[4,2]{0,1:T(2,128)S(1)}, f32[4,1,128,128]{3,2,1,0:T(8,128)S(1)}, s32[]{:T(128)}) %tuple.57), condition=%wide.while_cond, body=%wide.while_body.sunk | while | flops 2 | bytes 393333 | solution.py:22
  325.9 1.3 constant_dynamic-slice_fusion.11
  328.0 1.3 constant_dynamic-slice_fusion.11
  330.0 1.3 constant_dynamic-slice_fusion.11
  332.0 1.3 constant_dynamic-slice_fusion.11
  333.5 39.3 %custom-call.64 = f32[1,4,128,128]{2,3,1,0:T(8,128)S(1)} custom-call(f32[1,4,128,128]{3,2,1,0:T(8,128)S(1)} %bitcast.370), custom_call_target="InvertDiagBlocksLowerTriangular" | custom-call | tf_op jit(solution)/shard_map/while/body/eval_jaxpr/vmap(jit(_cho_solve))/triangular_solve | solution.py:22
  372.8 1.8 fusion.107
  374.6 0.7 copy.187
  375.5 0.8 fusion.106
  376.3 0.8 fusion.72
  380.1 0.7 fusion.70
  380.8 0.7 dynamic-slice_convert_fusion
  382.2 74.5 %all-gather.2.cloned.1.call-done = bf16[64,512,16]{1,2,0:T(8,128)(2,1)} async-done(((bf16[1,512,16]{1,2,0:T(8,128)(2,1)}), bf16[64,512,16]{1,2,0:T(8,128)(2,1)}) %all-gather.2.cloned.1.call-update) | async-done | bytes 1048592 | tf_op jit(solution)/shard_map/all_gather | solution.py:95
  456.6 1.0 slice.263
  457.7 1.5 fusion.111
  459.7 0.9 copy.188
  460.6 4.8 all-to-all-start
  466.0 4.4 all-to-all-done
  471.6 1.3 fusion.13
  473.2 3.5 psum.29
  476.7 29.2 %psum.30 = f32[20,440]{1,0:T(8,128)S(1)} all-reduce(f32[20,440]{1,0:T(8,128)S(1)} %psum.29), channel_id=1, replica_groups=mesh['x'=4,'z'=8,'c'=2,'blk'=4] {'z'}, use_global_device_ids=true, to_apply=%region_16.17 | all-reduce | flops 8800 | bytes 70400 | tf_op jit(solution)/shard_map/psum | solution.py:29
  505.9 16.1 %psum.31 = f32[20,440]{1,0:T(8,128)S(1)} all-reduce(f32[20,440]{1,0:T(8,128)S(1)} %psum.30), channel_id=1, replica_groups=mesh['x'=4,'z'=8,'c'=2,'blk'=4] {'x'}, use_global_device_ids=true, to_apply=%region_17.18 | all-reduce | flops 8800 | bytes 70400 | tf_op jit(solution)/shard_map/psum | solution.py:29
  522.9 0.8 gather_fusion.1
  527.1 36.7 %custom-call.65 = f32[20,20,20]{2,1,0:T(8,128)S(1)} custom-call(f32[20,20,20]{2,1,0:T(8,128)S(1)} %fusion.44), custom_call_target="Cholesky" | custom-call | tf_op jit(solution)/shard_map/jit(cholesky)/cholesky | solution.py:19
  564.1 30.9 %custom-call.66 = f32[20,1,20,20]{2,3,1,0:T(8,128)S(1)} custom-call(f32[20,1,20,20]{3,2,1,0:T(8,128)S(1)} %select_bitcast_fusion), custom_call_target="InvertDiagBlocksLowerTriangular" | custom-call | tf_op jit(solution)/shard_map/vmap(jit(_cho_solve))/triangular_solve | solution.py:22
  596.3 0.7 copy.213
  598.1 0.6 add_rsqrt_fusion.2
  598.8 0.7 multiply_bitcast_fusion.1
  (156 shorter events, 22.0 us)
Async XLA Ops:
  7.2 214.3 %all-reduce.3.cloned.1.call-start = ((), (), s32[]{:S(2)}) async-start(), calls=%async_computation.1 | async-start | bytes 13721600 | tf_op jit(solution)/shard_map/psum | solution.py:45
  16.3 0.7 copy-start.4
  16.4 440.3 %all-gather.2.cloned.1.call-start = ((), (), s32[]{:S(2)}) async-start(), calls=%async_computation.2 | async-start | bytes 1064960 | tf_op jit(solution)/shard_map/all_gather | solution.py:95
  372.8 86.4 %copy-start = (bf16[640,512]{1,0:T(8,128)(2,1)S(1)}, bf16[640,512]{1,0:T(8,128)(2,1)}, u32[]{:S(2)}) copy-start(bf16[640,512]{1,0:T(8,128)(2,1)} %param.4) | copy-start | bytes 1966084
  375.4 83.8 %copy-start.1 = (f32[640,5]{0,1:T(8,128)S(1)}, f32[640,5]{0,1:T(8,128)}, u32[]{:S(2)}) copy-start(f32[640,5]{0,1:T(8,128)} %get-tuple-element.137) | copy-start | bytes 38404
  377.9 92.7 %copy-start.2 = (s32[640]{0:T(1024)S(1)}, s32[640]{0:T(1024)}, u32[]{:S(2)}) copy-start(s32[640]{0:T(1024)} %param.6) | copy-start | bytes 7684
  379.9 91.7 %copy-start.3 = (f32[640,5]{0,1:T(8,128)S(1)}, f32[640,5]{0,1:T(8,128)}, u32[]{:S(2)}) copy-start(f32[640,5]{0,1:T(8,128)} %get-tuple-element.136) | copy-start | bytes 38404
  460.6 9.8 %all-to-all-start = ((f32[1,5,16,640]{3,0,1,2:T(1,128)}), f32[1,5,16,640]{3,0,1,2:T(1,128)S(1)}, u32[]{:S(2)}, u32[]{:S(2)}) async-start(f32[1,5,16,640]{3,0,1,2:T(1,128)} %copy.188), calls=%async_computation | async-start | bytes 409600 | tf_op jit(solution)/shard_map/all_to_all | solution.py:106
Sparse Core Ops, SparseCore 0:
  16.5 204.8 all-reduce.2
  380.9 75.6 all-gather.1

commit v2 on v1

--- a/solution.py
+++ b/solution.py
@@ -2,6 +2,7 @@
 import jax.numpy as jnp
 import numpy as np
 from jax import lax
+from jax.experimental import pallas as pl
 from jax.sharding import Mesh
 from jax.sharding import PartitionSpec as P
 
@@ -22,6 +23,43 @@
         return jax.scipy.linalg.cho_solve((factor, True), right_side)
 
     return jax.vmap(solve_single)(factors, right_sides)
+
+
+def _cholesky_solve_kernel(a_ref, b_ref, x_ref):
+    a = a_ref[...]
+    r = b_ref[...]
+    n = a.shape[0]
+    rows = jax.lax.broadcasted_iota(jnp.int32, r.shape, 0)
+    cols = jax.lax.broadcasted_iota(jnp.int32, (1,) + a.shape[1:], 1)
+    diags, columns = [], []
+    for j in range(n):
+        d = jnp.sqrt(a[j : j + 1, j : j + 1, :])
+        column = jnp.where(rows >= j, a[:, j : j + 1, :] / d, 0.0)
+        row = jnp.where(cols >= j, a[j : j + 1, :, :] / d, 0.0)
+        a = a - column * row
+        diags.append(d)
+        columns.append(column)
+    y = jnp.zeros_like(r)
+    for j in range(n):
+        yj = r[j : j + 1] / diags[j]
+        r = r - columns[j] * yj
+        y = jnp.where(rows == j, yj, y)
+    x = jnp.zeros_like(r)
+    for j in reversed(range(n)):
+        s = jnp.sum(jnp.where(rows > j, columns[j] * x, 0.0), axis=0, keepdims=True)
+        x = jnp.where(rows == j, (y[j : j + 1] - s) / diags[j], x)
+    x_ref[...] = x
+
+
+def cholesky_solve(systems, right_sides):
+    batch, n, _ = systems.shape
+    a = systems.transpose(1, 2, 0)
+    b = right_sides.T[:, None, :]
+    x = pl.pallas_call(
+        _cholesky_solve_kernel,
+        out_shape=jax.ShapeDtypeStruct((n, 1, batch), jnp.float32),
+    )(a, b)
+    return x[:, 0, :].T
 
 
 def psum_tree(value):
@@ -140,7 +178,7 @@
     train_grams = jnp.sum(fold_grams, axis=0)[None] - fold_grams
     train_cross = jnp.sum(fold_cross, axis=0)[None] - fold_cross
     shrunk = train_grams + total / 4.0 * jnp.eye(count_pred, dtype=jnp.float32)
-    weights = solve_batch(
+    weights = cholesky_solve(
         shrunk.reshape(-1, count_pred, count_pred), train_cross.reshape(-1, count_pred)
     )
     weights = weights.reshape(FOLDS, group, count_pred)

time: 611 us -> 552 us (0.903)
  other arithmetic: 210 us -> 143 us
    another operation x18 -> x14, other arithmetic: 116 us -> 79 us  [solve_batch(): factors = jnp.linalg.cholesky(systems)]
    another operation x6 -> x3, other arithmetic: 70.5 us -> 39.4 us  [solve_single(): return jax.scipy.linalg.cho_solve((factor, True), right_side)]
where the time goes in v2:
time: 552 us; the launch traced here: 547 us
  waiting for transfers between devices  283 us (51%)
  other arithmetic  143 us (26%)
  blocking collectives  53.2 us (10%)
  local copies, waits for them, and re-layouts  25.6 us (5%)
  between operations  19.2 us (3%)
  matrix products  15.8 us (3%)
    psum x1, waiting for transfers between devices, shards(): stats = lax.psum(stats, SAMP)  204 us
    another operation x14, other arithmetic, solve_batch(): factors = jnp.linalg.cholesky(systems)  79 us
    all_gather x1, waiting for transfers between devices, shards(): collected = lax.all_gather(owned, SAMP, axis=0, tiled=True)  75.1 us
    psum x3, blocking collectives, psum_tree(): value = lax.psum(value, name)  53.2 us
    another operation x3, other arithmetic, solve_single(): return jax.scipy.linalg.cho_solve((factor, True), right_side)  39.4 us
  transfers between devices with their start and end apart: 3, of which 3 were waited for; matrix products, arithmetic and copies ran while one was open for 0% of the time, Pallas kernels for 0%

profile of v2, /device:TPU:8, one launch (start us, length us, event | category | flops | bytes accessed | tf_op | source)
XLA Modules:
  0.0 547.0 jit_solution(8648238798382107826)
XLA Ops:
  7.2 1.4 copy.230
  8.6 1.3 convert_bitcast_fusion
  9.9 0.9 pad_maximum_fusion
  10.8 5.5 %fusion.2 = f32[5,529,529]{1,2,0:T(8,128)} fusion(bf16[640,529]{0,1:T(8,128)(2,1)S(1)} %pad_maximum_fusion, bf16[5,640]{1,0:T(8,128)(2,1)S(1)} %get-tuple-element.136), kind=kOutput, calls=%fused_computation.7 | convolution fusion | flops 1792675200 | bytes 6280340 | tf_op jit(solution)/shard_map/ri,krj->kij/dot_general | solution.py:82
  17.6 203.8 %all-reduce.3.cloned.1.call-done = f32[5,529,529]{1,2,0:T(8,128)} async-done(((f32[5,529,529]{1,2,0:T(8,128)}), f32[5,529,529]{1,2,0:T(8,128)}) %all-reduce.3.cloned.1.call-update) | async-done | bytes 5596836 | tf_op jit(solution)/shard_map/psum | solution.py:83
  221.4 1.5 slice_reduce_fusion.1
  223.4 0.9 fusion.100
  225.5 6.1 %fusion.101 = (f32[5,512,512]{1,2,0:T(8,128)}, f32[512,512]{0,1:T(8,128)S(1)}) fusion(f32[5,529,529]{1,2,0:T(8,128)} %all-reduce.3.cloned.1.call-done), kind=kLoop, calls=%fused_computation.211 | loop fusion | flops 1048576 | bytes 11534336 | tf_op jit(solution)/shard_map/slice | solution.py:84
  231.6 4.7 gather_fusion
  237.5 2.4 fusion.35
  240.5 11.7 %custom-call.46 = f32[1,128,128]{2,1,0:T(8,128)S(1)} custom-call(f32[1,128,128]{2,1,0:T(8,128)S(1)} %cholesky.264), custom_call_target="Cholesky" | custom-call | tf_op jit(solution)/shard_map/while/body/eval_jaxpr/jit(cholesky)/cholesky | solution.py:20
  252.3 9.8 %custom-call.47 = f32[1,1,128,128]{2,3,1,0:T(8,128)S(1)} custom-call(f32[1,1,128,128]{3,2,1,0:T(8,128)S(1)} %get-tuple-element.133), custom_call_target="InvertDiagBlocksLowerTriangular" | custom-call | tf_op jit(solution)/shard_map/while/body/eval_jaxpr/jit(cholesky)/cholesky | solution.py:20
  263.0 11.7 %custom-call.48 = f32[1,128,128]{2,1,0:T(8,128)S(1)} custom-call(f32[1,128,128]{2,1,0:T(8,128)S(1)} %cholesky.268), custom_call_target="Cholesky" | custom-call | tf_op jit(solution)/shard_map/while/body/eval_jaxpr/jit(cholesky)/cholesky | solution.py:20
  275.0 10.0 %custom-call.49 = f32[1,1,128,128]{2,3,1,0:T(8,128)S(1)} custom-call(f32[1,1,128,128]{3,2,1,0:T(8,128)S(1)} %get-tuple-element.131), custom_call_target="InvertDiagBlocksLowerTriangular" | custom-call | tf_op jit(solution)/shard_map/while/body/eval_jaxpr/jit(cholesky)/cholesky | solution.py:20
  285.9 11.7 %custom-call.50 = f32[1,128,128]{2,1,0:T(8,128)S(1)} custom-call(f32[1,128,128]{2,1,0:T(8,128)S(1)} %cholesky.273), custom_call_target="Cholesky" | custom-call | tf_op jit(solution)/shard_map/while/body/eval_jaxpr/jit(cholesky)/cholesky | solution.py:20
  297.8 9.8 %custom-call.51 = f32[1,1,128,128]{2,3,1,0:T(8,128)S(1)} custom-call(f32[1,1,128,128]{3,2,1,0:T(8,128)S(1)} %get-tuple-element.129), custom_call_target="InvertDiagBlocksLowerTriangular" | custom-call | tf_op jit(solution)/shard_map/while/body/eval_jaxpr/jit(cholesky)/cholesky | solution.py:20
  308.4 12.1 %custom-call.52 = f32[1,128,128]{2,1,0:T(8,128)S(1)} custom-call(f32[1,128,128]{2,1,0:T(8,128)S(1)} %fusion.21), custom_call_target="Cholesky" | custom-call | tf_op jit(solution)/shard_map/while/body/eval_jaxpr/jit(cholesky)/cholesky | solution.py:20
  320.6 0.6 compare_reduce_fusion.1
  321.3 0.7 compare_reduce_fusion
  321.9 0.7 compare_reduce_fusion.2
  325.3 8.1 %while.1 = (s32[]{:T(128)}, f32[1,512,512]{1,2,0:T(8,128)S(1)}, s32[4,2]{0,1:T(2,128)S(1)}, f32[4,1,128,128]{3,2,1,0:T(8,128)S(1)}, s32[]{:T(128)}) while((s32[]{:T(128)}, f32[1,512,512]{1,2,0:T(8,128)S(1)}, s32[4,2]{0,1:T(2,128)S(1)}, f32[4,1,128,128]{3,2,1,0:T(8,128)S(1)}, s32[]{:T(128)}) %tuple.56), condition=%wide.while_cond, body=%wide.while_body.sunk | while | flops 2 | bytes 393333 | solution.py:23
  325.9 1.3 constant_dynamic-slice_fusion.11
  328.0 1.3 constant_dynamic-slice_fusion.11
  330.0 1.3 constant_dynamic-slice_fusion.11
  332.0 1.3 constant_dynamic-slice_fusion.11
  333.5 39.3 %custom-call.53 = f32[1,4,128,128]{2,3,1,0:T(8,128)S(1)} custom-call(f32[1,4,128,128]{3,2,1,0:T(8,128)S(1)} %bitcast.352), custom_call_target="InvertDiagBlocksLowerTriangular" | custom-call | tf_op jit(solution)/shard_map/while/body/eval_jaxpr/vmap(jit(_cho_solve))/triangular_solve | solution.py:23
  372.8 1.8 fusion.99
  374.6 0.7 copy.241
  375.5 0.8 fusion.98
  376.3 0.8 fusion.65
  380.1 0.7 fusion.63
  380.8 0.7 dynamic-slice_convert_fusion
  381.5 75.1 %all-gather.2.cloned.1.call-done = bf16[64,512,16]{1,2,0:T(8,128)(2,1)} async-done(((bf16[1,512,16]{1,2,0:T(8,128)(2,1)}), bf16[64,512,16]{1,2,0:T(8,128)(2,1)}) %all-gather.2.cloned.1.call-update) | async-done | bytes 1048592 | tf_op jit(solution)/shard_map/all_gather | solution.py:133
  456.6 1.0 slice.245
  457.7 1.5 fusion.103
  459.7 0.9 copy.242
  460.6 4.8 all-to-all-start
  466.5 3.8 all-to-all-done
  471.6 1.4 fusion.13
  473.4 3.9 psum.29
  477.2 31.3 %psum.30 = f32[20,440]{0,1:T(8,128)S(1)} all-reduce(f32[20,440]{0,1:T(8,128)S(1)} %psum.29), channel_id=1, replica_groups=mesh['x'=4,'z'=8,'c'=2,'blk'=4] {'z'}, use_global_device_ids=true, to_apply=%region_16.17 | all-reduce | flops 8800 | bytes 70400 | tf_op jit(solution)/shard_map/psum | solution.py:67
  508.5 18.1 %psum.31 = f32[20,440]{0,1:T(8,128)S(1)} all-reduce(f32[20,440]{0,1:T(8,128)S(1)} %psum.30), channel_id=1, replica_groups=mesh['x'=4,'z'=8,'c'=2,'blk'=4] {'x'}, use_global_device_ids=true, to_apply=%region_17.18 | all-reduce | flops 8800 | bytes 70400 | tf_op jit(solution)/shard_map/psum | solution.py:67
  527.5 0.8 gather_fusion.1
  532.5 0.8 add_bitcast_fusion.a_ref
  533.3 2.4 shard_map.59
  535.7 0.8 copy.322
  536.9 0.7 copy.279
  539.3 0.7 multiply_bitcast_fusion.1
  (158 shorter events, 22.3 us)
Async XLA Ops:
  7.2 214.3 %all-reduce.3.cloned.1.call-start = ((), (), s32[]{:S(2)}) async-start(), calls=%async_computation.1 | async-start | bytes 13721600 | tf_op jit(solution)/shard_map/psum | solution.py:83
  16.3 0.7 copy-start.4
  16.4 440.3 %all-gather.2.cloned.1.call-start = ((), (), s32[]{:S(2)}) async-start(), calls=%async_computation.2 | async-start | bytes 1064960 | tf_op jit(solution)/shard_map/all_gather | solution.py:133
  372.8 86.4 %copy-start = (bf16[640,512]{1,0:T(8,128)(2,1)S(1)}, bf16[640,512]{1,0:T(8,128)(2,1)}, u32[]{:S(2)}) copy-start(bf16[640,512]{1,0:T(8,128)(2,1)} %param.4) | copy-start | bytes 1966084
  375.4 83.8 %copy-start.1 = (f32[640,5]{0,1:T(8,128)S(1)}, f32[640,5]{0,1:T(8,128)}, u32[]{:S(2)}) copy-start(f32[640,5]{0,1:T(8,128)} %get-tuple-element.135) | copy-start | bytes 38404
  377.9 92.7 %copy-start.2 = (s32[640]{0:T(1024)S(1)}, s32[640]{0:T(1024)}, u32[]{:S(2)}) copy-start(s32[640]{0:T(1024)} %param.6) | copy-start | bytes 7684
  379.9 91.7 %copy-start.3 = (f32[640,5]{0,1:T(8,128)S(1)}, f32[640,5]{0,1:T(8,128)}, u32[]{:S(2)}) copy-start(f32[640,5]{0,1:T(8,128)} %get-tuple-element.134) | copy-start | bytes 38404
  460.6 9.8 %all-to-all-start = ((f32[1,5,16,640]{3,0,1,2:T(1,128)}), f32[1,5,16,640]{3,0,1,2:T(1,128)S(1)}, u32[]{:S(2)}, u32[]{:S(2)}) async-start(f32[1,5,16,640]{3,0,1,2:T(1,128)} %copy.242), calls=%async_computation | async-start | bytes 409600 | tf_op jit(solution)/shard_map/all_to_all | solution.py:144
Sparse Core Ops, SparseCore 0:
  16.5 204.8 all-reduce.2
  380.9 75.6 all-gather.1

commit v3 on v2

--- a/solution.py
+++ b/solution.py
@@ -114,9 +114,9 @@
         return (system, target)
 
     systems_count = FOLDS * SHRINK
-    samp_size = lax.axis_size(SAMP)
-    per_device = -(-systems_count // samp_size)
-    first = lax.axis_index(SAMP) * per_device
+    slots = lax.axis_size(("x", "z"))
+    per_device = -(-systems_count // slots)
+    first = lax.axis_index(("x", "z")) * per_device
 
     def solve_own(offset):
         which = jnp.minimum(first + offset, systems_count - 1)
@@ -130,7 +130,8 @@
         return (scale[:, None] * beta).astype(jnp.bfloat16)
 
     owned = lax.map(solve_own, jnp.arange(per_device, dtype=jnp.int32))
-    collected = lax.all_gather(owned, SAMP, axis=0, tiled=True)
+    collected = lax.all_gather(owned, "z", axis=0, tiled=True)
+    collected = lax.all_gather(collected, "x", axis=0, tiled=True)
     coef = collected[:systems_count].reshape(FOLDS, SHRINK, width, traits_count)
     coef_flat = coef.transpose(2, 0, 1, 3).reshape(width, FOLDS * SHRINK * traits_count)
     shift = jnp.einsum("v,klvt->klt", mean, coef.astype(jnp.float32), precision=HIGH)

time: 552 us -> 511 us (0.926)
  waiting for transfers between devices: 283 us -> 206 us
  blocking collectives: 53.2 us -> 89.6 us
    all_gather x1 -> x0, waiting for transfers between devices: 75.1 us -> none  [shards(): collected = lax.all_gather(owned, SAMP, axis=0, tiled=True)]
    all_gather x0 -> x2, blocking collectives: none -> 37.4 us  [the longest x1 24.6 us: shards(): collected = lax.all_gather(owned, 'z', axis=0, tiled=True)]
  transfers between devices with their start and end apart: 3 -> 2, of which waited for: 3 -> 2; matrix products, arithmetic and copies ran while one was open for 0% -> 0% of each run, Pallas kernels for 0% -> 0%
where the time goes in v3:
time: 511 us; the launch traced here: 506 us
  waiting for transfers between devices  206 us (40%)
  other arithmetic  143 us (28%)
  blocking collectives  89.6 us (18%)
  local copies, waits for them, and re-layouts  24.6 us (5%)
  between operations  19.2 us (4%)
  matrix products  15.8 us (3%)
    psum x1, waiting for transfers between devices, shards(): stats = lax.psum(stats, SAMP)  202 us
    another operation x14, other arithmetic, solve_batch(): factors = jnp.linalg.cholesky(systems)  79 us
    psum x3, blocking collectives, psum_tree(): value = lax.psum(value, name)  52.2 us
    another operation x3, other arithmetic, solve_single(): return jax.scipy.linalg.cho_solve((factor, True), right_side)  39.4 us
    all_gather x1, blocking collectives, shards(): collected = lax.all_gather(owned, 'z', axis=0, tiled=True)  24.6 us
    all_gather x1, blocking collectives, shards(): collected = lax.all_gather(collected, 'x', axis=0, tiled=True)  12.8 us
  transfers between devices with their start and end apart: 2, of which 2 were waited for; matrix products, arithmetic and copies ran while one was open for 0% of the time, Pallas kernels for 0%

profile of v3, /device:TPU:8, one launch (start us, length us, event | category | flops | bytes accessed | tf_op | source)
XLA Modules:
  0.0 506.0 jit_solution(10249792228752019013)
XLA Ops:
  7.2 1.4 copy.230
  8.6 1.3 convert_bitcast_fusion
  9.9 0.9 pad_maximum_fusion
  10.8 5.5 %fusion.2 = f32[5,529,529]{1,2,0:T(8,128)} fusion(bf16[640,529]{0,1:T(8,128)(2,1)S(1)} %pad_maximum_fusion, bf16[5,640]{1,0:T(8,128)(2,1)S(1)} %get-tuple-element.136), kind=kOutput, calls=%fused_computation.7 | convolution fusion | flops 1792675200 | bytes 6280340 | tf_op jit(solution)/shard_map/ri,krj->kij/dot_general | solution.py:82
  17.0 0.7 fusion.89
  17.7 1.3 dynamic-slice_convert_fusion
  19.0 202.5 %all-reduce.3.cloned.1.call-done = f32[5,529,529]{1,2,0:T(8,128)} async-done(((f32[5,529,529]{1,2,0:T(8,128)}), f32[5,529,529]{1,2,0:T(8,128)}) %all-reduce.3.cloned.1.call-update) | async-done | bytes 5596836 | tf_op jit(solution)/shard_map/psum | solution.py:83
  221.5 1.5 slice_reduce_fusion.1
  223.5 0.9 fusion.100
  225.6 6.1 %fusion.101 = (f32[5,512,512]{1,2,0:T(8,128)}, f32[512,512]{0,1:T(8,128)S(1)}) fusion(f32[5,529,529]{1,2,0:T(8,128)} %all-reduce.3.cloned.1.call-done), kind=kLoop, calls=%fused_computation.211 | loop fusion | flops 1048576 | bytes 11534336 | tf_op jit(solution)/shard_map/slice | solution.py:84
  231.7 4.7 gather_fusion
  237.6 2.4 fusion.35
  240.6 11.7 %custom-call.46 = f32[1,128,128]{2,1,0:T(8,128)S(1)} custom-call(f32[1,128,128]{2,1,0:T(8,128)S(1)} %cholesky.264), custom_call_target="Cholesky" | custom-call | tf_op jit(solution)/shard_map/while/body/eval_jaxpr/jit(cholesky)/cholesky | solution.py:20
  252.5 9.8 %custom-call.47 = f32[1,1,128,128]{2,3,1,0:T(8,128)S(1)} custom-call(f32[1,1,128,128]{3,2,1,0:T(8,128)S(1)} %get-tuple-element.133), custom_call_target="InvertDiagBlocksLowerTriangular" | custom-call | tf_op jit(solution)/shard_map/while/body/eval_jaxpr/jit(cholesky)/cholesky | solution.py:20
  263.1 11.7 %custom-call.48 = f32[1,128,128]{2,1,0:T(8,128)S(1)} custom-call(f32[1,128,128]{2,1,0:T(8,128)S(1)} %cholesky.268), custom_call_target="Cholesky" | custom-call | tf_op jit(solution)/shard_map/while/body/eval_jaxpr/jit(cholesky)/cholesky | solution.py:20
  275.1 10.0 %custom-call.49 = f32[1,1,128,128]{2,3,1,0:T(8,128)S(1)} custom-call(f32[1,1,128,128]{3,2,1,0:T(8,128)S(1)} %get-tuple-element.131), custom_call_target="InvertDiagBlocksLowerTriangular" | custom-call | tf_op jit(solution)/shard_map/while/body/eval_jaxpr/jit(cholesky)/cholesky | solution.py:20
  286.0 11.7 %custom-call.50 = f32[1,128,128]{2,1,0:T(8,128)S(1)} custom-call(f32[1,128,128]{2,1,0:T(8,128)S(1)} %cholesky.273), custom_call_target="Cholesky" | custom-call | tf_op jit(solution)/shard_map/while/body/eval_jaxpr/jit(cholesky)/cholesky | solution.py:20
  297.9 9.8 %custom-call.51 = f32[1,1,128,128]{2,3,1,0:T(8,128)S(1)} custom-call(f32[1,1,128,128]{3,2,1,0:T(8,128)S(1)} %get-tuple-element.129), custom_call_target="InvertDiagBlocksLowerTriangular" | custom-call | tf_op jit(solution)/shard_map/while/body/eval_jaxpr/jit(cholesky)/cholesky | solution.py:20
  308.5 12.1 %custom-call.52 = f32[1,128,128]{2,1,0:T(8,128)S(1)} custom-call(f32[1,128,128]{2,1,0:T(8,128)S(1)} %fusion.21), custom_call_target="Cholesky" | custom-call | tf_op jit(solution)/shard_map/while/body/eval_jaxpr/jit(cholesky)/cholesky | solution.py:20
  320.7 0.6 compare_reduce_fusion.1
  321.4 0.7 compare_reduce_fusion
  322.0 0.7 compare_reduce_fusion.2
  325.4 8.1 %while.1 = (s32[]{:T(128)}, f32[1,512,512]{1,2,0:T(8,128)S(1)}, s32[4,2]{0,1:T(2,128)S(1)}, f32[4,1,128,128]{3,2,1,0:T(8,128)S(1)}, s32[]{:T(128)}) while((s32[]{:T(128)}, f32[1,512,512]{1,2,0:T(8,128)S(1)}, s32[4,2]{0,1:T(2,128)S(1)}, f32[4,1,128,128]{3,2,1,0:T(8,128)S(1)}, s32[]{:T(128)}) %tuple.56), condition=%wide.while_cond, body=%wide.while_body.sunk | while | flops 2 | bytes 393333 | solution.py:23
  326.1 1.3 constant_dynamic-slice_fusion.11
  328.1 1.3 constant_dynamic-slice_fusion.11
  330.1 1.3 constant_dynamic-slice_fusion.11
  332.2 1.3 constant_dynamic-slice_fusion.11
  333.6 39.3 %custom-call.53 = f32[1,4,128,128]{2,3,1,0:T(8,128)S(1)} custom-call(f32[1,4,128,128]{3,2,1,0:T(8,128)S(1)} %bitcast.352), custom_call_target="InvertDiagBlocksLowerTriangular" | custom-call | tf_op jit(solution)/shard_map/while/body/eval_jaxpr/vmap(jit(_cho_solve))/triangular_solve | solution.py:23
  372.9 1.8 fusion.99
  374.8 0.7 copy.241
  375.6 0.8 fusion.98
  376.4 0.8 fusion.65
  380.3 24.6 %all_gather.6 = bf16[8,512,16]{1,2,0:T(8,128)(2,1)S(1)} all-gather(bf16[1,512,16]{1,2,0:T(8,128)(2,1)S(1)} %fusion.63), channel_id=1, replica_groups=mesh['x'=4,'z'=8,'c'=2,'blk'=4] {'z'}, dimensions={0}, use_global_device_ids=true | all-gather | bytes 147456 | tf_op jit(solution)/shard_map/all_gather | solution.py:133
  404.9 12.8 %all_gather.7 = bf16[32,512,16]{1,2,0:T(8,128)(2,1)S(1)} all-gather(bf16[8,512,16]{1,2,0:T(8,128)(2,1)S(1)} %all_gather.6), channel_id=1, replica_groups=mesh['x'=4,'z'=8,'c'=2,'blk'=4] {'x'}, dimensions={0}, use_global_device_ids=true | all-gather | bytes 655360 | tf_op jit(solution)/shard_map/all_gather | solution.py:134
  417.7 1.5 fusion.103
  419.7 0.9 copy.242
  420.6 4.8 all-to-all-start
  426.5 3.8 all-to-all-done
  431.6 1.4 fusion.13
  433.3 3.9 psum.29
  437.2 30.3 %psum.30 = f32[20,440]{0,1:T(8,128)S(1)} all-reduce(f32[20,440]{0,1:T(8,128)S(1)} %psum.29), channel_id=1, replica_groups=mesh['x'=4,'z'=8,'c'=2,'blk'=4] {'z'}, use_global_device_ids=true, to_apply=%region_16.17 | all-reduce | flops 8800 | bytes 70400 | tf_op jit(solution)/shard_map/psum | solution.py:67
  467.5 18.0 %psum.31 = f32[20,440]{0,1:T(8,128)S(1)} all-reduce(f32[20,440]{0,1:T(8,128)S(1)} %psum.30), channel_id=1, replica_groups=mesh['x'=4,'z'=8,'c'=2,'blk'=4] {'x'}, use_global_device_ids=true, to_apply=%region_17.18 | all-reduce | flops 8800 | bytes 70400 | tf_op jit(solution)/shard_map/psum | solution.py:67
  486.5 0.8 gather_fusion.1
  491.4 0.8 add_bitcast_fusion.a_ref
  492.2 2.4 shard_map.59
  494.6 0.8 copy.322
  495.8 0.7 copy.279
  498.2 0.7 multiply_bitcast_fusion.1
  (159 shorter events, 21.9 us)
Async XLA Ops:
  7.2 214.3 %all-reduce.3.cloned.1.call-start = ((), (), s32[]{:S(2)}) async-start(), calls=%async_computation.1 | async-start | bytes 13721600 | tf_op jit(solution)/shard_map/psum | solution.py:83
  16.4 0.7 copy-start.5
  372.9 46.3 %copy-start = (bf16[640,512]{1,0:T(8,128)(2,1)S(1)}, bf16[640,512]{1,0:T(8,128)(2,1)}, u32[]{:S(2)}) copy-start(bf16[640,512]{1,0:T(8,128)(2,1)} %param.4) | copy-start | bytes 1966084
  375.5 43.7 %copy-start.1 = (f32[640,5]{0,1:T(8,128)S(1)}, f32[640,5]{0,1:T(8,128)}, u32[]{:S(2)}) copy-start(f32[640,5]{0,1:T(8,128)} %get-tuple-element.135) | copy-start | bytes 38404
  378.4 52.0 %copy-start.2 = (f32[4,640]{1,0:T(4,128)S(1)}, f32[4,640]{1,0:T(4,128)}, u32[]{:S(2)}) copy-start(f32[4,640]{1,0:T(4,128)} %dynamic-slice_convert_fusion) | copy-start | bytes 30724
  379.4 51.1 %copy-start.3 = (s32[640]{0:T(1024)S(1)}, s32[640]{0:T(1024)}, u32[]{:S(2)}) copy-start(s32[640]{0:T(1024)} %param.6) | copy-start | bytes 7684
  417.6 13.9 %copy-start.4 = (f32[640,5]{0,1:T(8,128)S(1)}, f32[640,5]{0,1:T(8,128)}, u32[]{:S(2)}) copy-start(f32[640,5]{0,1:T(8,128)} %get-tuple-element.134) | copy-start | bytes 38404
  420.6 9.7 %all-to-all-start = ((f32[1,5,16,640]{3,0,1,2:T(1,128)}), f32[1,5,16,640]{3,0,1,2:T(1,128)S(1)}, u32[]{:S(2)}, u32[]{:S(2)}) async-start(f32[1,5,16,640]{3,0,1,2:T(1,128)} %copy.242), calls=%async_computation | async-start | bytes 409600 | tf_op jit(solution)/shard_map/all_to_all | solution.py:145
Sparse Core Ops, SparseCore 0:
  16.5 204.9 all-reduce.2

commit v4 on v3

--- a/solution.py
+++ b/solution.py
@@ -68,6 +68,41 @@
     return value
 
 
+def reduce_scatter_a2a(value, name):
+    n = lax.axis_size(name)
+    value = value.reshape((n, value.shape[0] // n) + value.shape[1:])
+    return jnp.sum(lax.all_to_all(value, name, 0, 0, tiled=True), axis=0)
+
+
+def psum_symmetric(stats):
+    count, size, _ = stats.shape
+    upper = jnp.triu(jnp.ones((size, size), jnp.bool_))
+    pairs = count // 2
+    packed = [jnp.where(upper, stats[2 * i], stats[2 * i + 1]) for i in range(pairs)]
+    packed += [stats[i] for i in range(2 * pairs, count)]
+    diagonals = [jnp.diagonal(stats[2 * i + 1])[None] for i in range(pairs)]
+    rows = jnp.concatenate([p for p in packed] + diagonals, axis=0)
+    parts = lax.axis_size(SAMP)
+    padded = -(-rows.shape[0] // parts) * parts
+    rows = jnp.pad(rows, ((0, padded - rows.shape[0]), (0, 0)))
+    for name in ("c", "z", "x"):
+        rows = reduce_scatter_a2a(rows, name)
+    for name in ("x", "z", "c"):
+        rows = lax.all_gather(rows, name, axis=0, tiled=True)
+    squares = len(packed)
+    blocks = rows[: squares * size].reshape(squares, size, size)
+    diagonals = rows[squares * size : squares * size + pairs]
+    eye = jnp.eye(size, dtype=jnp.bool_)
+    out = []
+    for i in range(pairs):
+        block = blocks[i]
+        first = jnp.where(upper, block, block.T)
+        second = jnp.where(eye, diagonals[i][None, :], jnp.where(upper, block.T, block))
+        out += [first, second]
+    out += [blocks[i] for i in range(pairs, squares)]
+    return jnp.stack(out)
+
+
 def shards(dosages, traits, folds):
     rows, width = dosages.shape
     traits_count = traits.shape[0]
@@ -80,7 +115,7 @@
     )
     weighted = mask_half[:, :, None] * augmented[None]
     stats = jnp.einsum("ri,krj->kij", augmented, weighted, preferred_element_type=jnp.float32)
-    stats = lax.psum(stats, SAMP)
+    stats = psum_symmetric(stats)
     gram = stats[:, :width, :width]
     sums = stats[:, :width, width]
     counts = stats[:, width, width]

time: 511 us -> 539 us (1.055)
  waiting for transfers between devices: 206 us -> 55.7 us
  blocking collectives: 89.6 us -> 186 us
  local copies, waits for them, and re-layouts: 24.6 us -> 91.3 us
  other arithmetic: 143 us -> 156 us
    psum x1 -> x0, waiting for transfers between devices: 202 us -> none  [shards(): stats = lax.psum(stats, SAMP)]
    all_to_all x0 -> x3, blocking collectives: none -> 79.6 us  [reduce_scatter_a2a(): return jnp.sum(lax.all_to_all(value, name, 0, 0, tiled=True), axis=0)]
    all_gather x0 -> x2, waiting for transfers between devices: none -> 51.9 us  [psum_symmetric(): rows = lax.all_gather(rows, name, axis=0, tiled=True)]
    gather x0 -> x2, local copies, waits for them, and re-layouts: none -> 15.2 us  [psum_symmetric(): diagonals = [jnp.diagonal(stats[2 * i + 1])[None] for i in range(pairs)]]
    reshape x0 -> x5, local copies, waits for them, and re-layouts: none -> 12.9 us  [reduce_scatter_a2a(): value = value.reshape((n, value.shape[0] // n) + value.shape[1:])]
    all_gather x0 -> x1, blocking collectives: none -> 12.4 us  [psum_symmetric(): rows = lax.all_gather(rows, name, axis=0, tiled=True)]
    unnamed x14 -> x18, local copies, waits for them, and re-layouts: 2.66 us -> 12.5 us
    unnamed x1 -> x5, other arithmetic: 0.01 us -> 8.58 us
  transfers between devices with their start and end apart: 2 -> 3, of which waited for: 2 -> 3; matrix products, arithmetic and copies ran while one was open for 0% -> 0% of each run, Pallas kernels for 0% -> 0%
where the time goes in v4:
time: 539 us; the launch traced here: 529 us
  blocking collectives  186 us (35%)
  other arithmetic  156 us (29%)
  local copies, waits for them, and re-layouts  91.3 us (17%)
  waiting for transfers between devices  55.7 us (10%)
  between operations  19.8 us (4%)
  matrix products  13.8 us (3%)
    all_to_all x3, blocking collectives, reduce_scatter_a2a(): return jnp.sum(lax.all_to_all(value, name, 0, 0, tiled=True), axis=0)  79.6 us
    another operation x14, other arithmetic, solve_batch(): factors = jnp.linalg.cholesky(systems)  78.8 us
    psum x3, blocking collectives, psum_tree(): value = lax.psum(value, name)  54.5 us
    all_gather x2, waiting for transfers between devices, psum_symmetric(): rows = lax.all_gather(rows, name, axis=0, tiled=True)  51.9 us
    another operation x3, other arithmetic, solve_single(): return jax.scipy.linalg.cho_solve((factor, True), right_side)  40.3 us
    all_gather x1, blocking collectives, shards(): collected = lax.all_gather(owned, 'z', axis=0, tiled=True)  26 us
    gather x2, local copies, waits for them, and re-layouts, psum_symmetric(): diagonals = [jnp.diagonal(stats[2 * i + 1])[None] for i in range(pairs)]  15.2 us
    all_gather x1, blocking collectives, shards(): collected = lax.all_gather(collected, 'x', axis=0, tiled=True)  13.1 us
  transfers between devices with their start and end apart: 3, of which 3 were waited for; matrix products, arithmetic and copies ran while one was open for 0% of the time, Pallas kernels for 0%

profile of v4, /device:TPU:8, one launch (start us, length us, event | category | flops | bytes accessed | tf_op | source)
XLA Modules:
  0.0 529.4 jit_solution(11988057698130180875)
XLA Ops:
  9.6 3.5 fusion.2
  14.4 1.8 fusion.8
  16.2 7.6 %gather_fusion = f32[529]{0:T(1024)S(1)} fusion(f32[529,529]{0,1:T(8,128)S(1)} %get-tuple-element.132, s32[529]{0:T(1024)S(1)} %or_reduce_fusion), kind=kCustom, calls=%fused_computation | custom fusion | bytes 8464 | tf_op jit(solution)/shard_map/jit(diagonal)/cond/branch_0_fun/gather | solution.py:83
  24.0 7.6 %gather_fusion.1 = f32[529]{0:T(1024)S(1)} fusion(f32[529,529]{0,1:T(8,128)S(1)} %get-tuple-element.130, s32[529]{0:T(1024)S(1)} %or_reduce_fusion), kind=kCustom, calls=%fused_computation.1 | custom fusion | bytes 8464 | tf_op jit(solution)/shard_map/jit(diagonal)/cond/branch_0_fun/gather | solution.py:83
  31.7 4.6 concatenate.58
  36.4 4.0 pad.5
  40.4 5.8 %reshape.723 = f32[2,800,529]{1,0,2:T(2,128)} reshape(f32[1600,529]{0,1:T(8,128)} %pad.5) | data formatting | bytes 6771200 | tf_op jit(solution)/shard_map/reshape | solution.py:73
  46.2 2.3 copy.267
  48.5 7.9 %all_to_all.30 = f32[2,800,529]{1,2,0:T(8,128)} all-to-all(f32[2,800,529]{1,2,0:T(8,128)S(1)} %copy.267), channel_id=1, replica_groups=mesh['x'=4,'z'=8,'c'=2,'blk'=4] {'c'}, dimensions={0} | all-to-all | bytes 6771200 | tf_op jit(solution)/shard_map/all_to_all | solution.py:74
  56.4 3.9 reduce_sum.124
  60.2 2.4 reshape.724
  62.6 2.3 copy.268
  64.9 60.7 %all_to_all.31 = f32[8,100,529]{2,1,0:T(8,128)S(1)} all-to-all(f32[8,100,529]{2,1,0:T(8,128)} %copy.268), channel_id=1, replica_groups=mesh['x'=4,'z'=8,'c'=2,'blk'=4] {'z'}, dimensions={0} | all-to-all | bytes 3385600 | tf_op jit(solution)/shard_map/all_to_all | solution.py:74
  125.8 11.1 %all_to_all.32 = f32[4,25,529]{2,1,0:T(8,128)S(1)} all-to-all(f32[4,25,529]{2,1,0:T(8,128)S(1)} %reshape.725), channel_id=1, replica_groups=mesh['x'=4,'z'=8,'c'=2,'blk'=4] {'x'}, dimensions={0} | all-to-all | bytes 423200 | tf_op jit(solution)/shard_map/all_to_all | solution.py:74
  136.9 12.4 %all-gather = f32[4,25,529]{2,1,0:T(8,128)S(1)} all-gather(f32[1,25,529]{2,1,0:T(8,128)S(1)} %bitcast.387), channel_id=1, replica_groups=mesh['x'=4,'z'=8,'c'=2,'blk'=4] {'x'}, dimensions={0}, use_global_device_ids=true | all-gather | bytes 264500 | tf_op jit(solution)/shard_map/all_gather | solution.py:91
  150.4 35.9 %all-gather.6.cloned.1.call-done = f32[8,100,529]{2,1,0:T(8,128)} async-done(((f32[1,100,529]{2,1,0:T(8,128)}), f32[8,100,529]{2,1,0:T(8,128)}) %all-gather.6.cloned.1.call-update) | async-done | bytes 1692816 | tf_op jit(solution)/shard_map/all_gather | solution.py:91
  186.2 1.7 reshape.837
  187.9 2.0 copy.356
  191.1 16.0 %all-gather.8.cloned.1.call-done = f32[2,800,529]{1,2,0:T(8,128)} async-done(((f32[1,800,529]{1,2,0:T(8,128)}), f32[2,800,529]{1,2,0:T(8,128)}) %all-gather.8.cloned.1.call-update) | async-done | bytes 3385616 | tf_op jit(solution)/shard_map/all_gather | solution.py:91
  207.2 5.9 %copy.272 = f32[2,800,529]{1,0,2:T(2,128)} copy(f32[2,800,529]{1,2,0:T(8,128)} %all-gather.8.cloned.1.call-done) | data formatting | bytes 6771200 | tf_op jit(solution)/shard_map/all_gather | solution.py:91
  213.1 5.5 %reshape.818 = f32[1600,529]{0,1:T(8,128)} reshape(f32[2,800,529]{1,0,2:T(2,128)} %copy.272) | data formatting | bytes 6771200
  218.6 3.4 fusion.107
  223.8 2.6 bitcast_dynamic-update-slice_fusion.4
  226.4 1.8 copy.274
  228.2 2.8 bitcast_dynamic-update-slice_fusion.3
  231.0 1.6 bitcast_dynamic-update-slice_fusion.2
  232.6 1.6 bitcast_dynamic-update-slice_fusion.1
  239.0 6.1 %fusion.106 = (f32[5,512,512]{1,2,0:T(8,128)}, f32[512,512]{0,1:T(8,128)S(1)}) fusion(f32[5,529,529]{1,2,0:T(8,128)} %fusion.7), kind=kLoop, calls=%fused_computation.238 | loop fusion | flops 1048576 | bytes 11534336 | tf_op jit(solution)/shard_map/slice | solution.py:119
  245.1 2.9 fusion.104
  249.9 5.0 gather_fusion.2
  256.1 2.4 fusion.40
  259.1 11.7 %custom-call.46 = f32[1,128,128]{2,1,0:T(8,128)S(1)} custom-call(f32[1,128,128]{2,1,0:T(8,128)S(1)} %cholesky.264), custom_call_target="Cholesky" | custom-call | tf_op jit(solution)/shard_map/while/body/eval_jaxpr/jit(cholesky)/cholesky | solution.py:20
  270.8 9.8 %custom-call.47 = f32[1,1,128,128]{2,3,1,0:T(8,128)S(1)} custom-call(f32[1,1,128,128]{3,2,1,0:T(8,128)S(1)} %get-tuple-element.142), custom_call_target="InvertDiagBlocksLowerTriangular" | custom-call | tf_op jit(solution)/shard_map/while/body/eval_jaxpr/jit(cholesky)/cholesky | solution.py:20
  281.4 11.7 %custom-call.48 = f32[1,128,128]{2,1,0:T(8,128)S(1)} custom-call(f32[1,128,128]{2,1,0:T(8,128)S(1)} %cholesky.268), custom_call_target="Cholesky" | custom-call | tf_op jit(solution)/shard_map/while/body/eval_jaxpr/jit(cholesky)/cholesky | solution.py:20
  293.5 10.0 %custom-call.49 = f32[1,1,128,128]{2,3,1,0:T(8,128)S(1)} custom-call(f32[1,1,128,128]{3,2,1,0:T(8,128)S(1)} %get-tuple-element.140), custom_call_target="InvertDiagBlocksLowerTriangular" | custom-call | tf_op jit(solution)/shard_map/while/body/eval_jaxpr/jit(cholesky)/cholesky | solution.py:20
  304.5 11.7 %custom-call.50 = f32[1,128,128]{2,1,0:T(8,128)S(1)} custom-call(f32[1,128,128]{2,1,0:T(8,128)S(1)} %cholesky.273), custom_call_target="Cholesky" | custom-call | tf_op jit(solution)/shard_map/while/body/eval_jaxpr/jit(cholesky)/cholesky | solution.py:20
  316.3 9.8 %custom-call.51 = f32[1,1,128,128]{2,3,1,0:T(8,128)S(1)} custom-call(f32[1,1,128,128]{3,2,1,0:T(8,128)S(1)} %get-tuple-element.138), custom_call_target="InvertDiagBlocksLowerTriangular" | custom-call | tf_op jit(solution)/shard_map/while/body/eval_jaxpr/jit(cholesky)/cholesky | solution.py:20
  326.9 11.9 %custom-call.52 = f32[1,128,128]{2,1,0:T(8,128)S(1)} custom-call(f32[1,128,128]{2,1,0:T(8,128)S(1)} %fusion.26), custom_call_target="Cholesky" | custom-call | tf_op jit(solution)/shard_map/while/body/eval_jaxpr/jit(cholesky)/cholesky | solution.py:20
  344.9 11.4 %while.1 = (s32[]{:T(128)}, f32[1,512,512]{1,2,0:T(8,128)S(1)}, s32[4,2]{0,1:T(2,128)S(1)}, f32[4,1,128,128]{3,2,1,0:T(8,128)}, s32[]{:T(128)}) while((s32[]{:T(128)}, f32[1,512,512]{1,2,0:T(8,128)S(1)}, s32[4,2]{0,1:T(2,128)S(1)}, f32[4,1,128,128]{3,2,1,0:T(8,128)}, s32[]{:T(128)}) %tuple.61), condition=%wide.while_cond, body=%wide.while_body.sunk | while | flops 2 | bytes 393833 | solution.py:23
  356.2 40.1 %custom-call.53 = f32[1,4,128,128]{2,3,1,0:T(8,128)S(1)} custom-call(f32[1,4,128,128]{3,2,1,0:T(8,128)} %bitcast.408), custom_call_target="InvertDiagBlocksLowerTriangular" | custom-call | tf_op jit(solution)/shard_map/while/body/eval_jaxpr/vmap(jit(_cho_solve))/triangular_solve | solution.py:23
  399.4 26.0 %all_gather.18 = bf16[8,512,16]{1,2,0:T(8,128)(2,1)S(1)} all-gather(bf16[1,512,16]{1,2,0:T(8,128)(2,1)S(1)} %fusion.68), channel_id=1, replica_groups=mesh['x'=4,'z'=8,'c'=2,'blk'=4] {'z'}, dimensions={0}, use_global_device_ids=true | all-gather | bytes 147456 | tf_op jit(solution)/shard_map/all_gather | solution.py:168
  425.5 13.1 %all_gather.19 = bf16[32,512,16]{1,2,0:T(8,128)(2,1)S(1)} all-gather(bf16[8,512,16]{1,2,0:T(8,128)(2,1)S(1)} %all_gather.18), channel_id=1, replica_groups=mesh['x'=4,'z'=8,'c'=2,'blk'=4] {'x'}, dimensions={0}, use_global_device_ids=true | all-gather | bytes 655360 | tf_op jit(solution)/shard_map/all_gather | solution.py:169
  441.5 4.8 all-to-all-start.3
  447.5 3.7 all-to-all-done.3
  454.2 3.9 psum.21
  458.1 31.4 %psum.22 = f32[20,440]{0,1:T(8,128)S(1)} all-reduce(f32[20,440]{0,1:T(8,128)S(1)} %psum.21), channel_id=1, replica_groups=mesh['x'=4,'z'=8,'c'=2,'blk'=4] {'z'}, use_global_device_ids=true, to_apply=%region_18.19 | all-reduce | flops 8800 | bytes 70400 | tf_op jit(solution)/shard_map/psum | solution.py:67
  489.5 19.2 %psum.23 = f32[20,440]{0,1:T(8,128)S(1)} all-reduce(f32[20,440]{0,1:T(8,128)S(1)} %psum.22), channel_id=1, replica_groups=mesh['x'=4,'z'=8,'c'=2,'blk'=4] {'x'}, use_global_device_ids=true, to_apply=%region_19.20 | all-reduce | flops 8800 | bytes 70400 | tf_op jit(solution)/shard_map/psum | solution.py:67
  514.4 2.4 shard_map.59
  (198 shorter events, 53.5 us)
Async XLA Ops:
  7.2 2.2 copy-start.4
  7.2 179.1 %all-gather.6.cloned.1.call-start = ((), (), s32[]{:S(2)}) async-start(), calls=%async_computation.4 | async-start | bytes 2396160 | tf_op jit(solution)/shard_map/all_gather | solution.py:91
  24.0 7.8 %copy-start.1 = (f32[529,529]{0,1:T(8,128)S(1)}, f32[529,529]{0,1:T(8,128)}, u32[]{:S(2)}) copy-start(f32[529,529]{0,1:T(8,128)} %get-tuple-element.131) | copy-start | bytes 3358096
  150.1 57.0 %all-gather.8.cloned.1.call-start = ((), (), s32[]{:S(2)}) async-start(), calls=%async_computation.5 | async-start | bytes 5763072 | tf_op jit(solution)/shard_map/all_gather | solution.py:91
  189.9 0.7 copy-start.5
  228.2 2.8 copy-start
  398.4 41.7 %copy-start.2 = (bf16[640,512]{1,0:T(8,128)(2,1)S(1)}, bf16[640,512]{1,0:T(8,128)(2,1)}, u32[]{:S(2)}) copy-start(bf16[640,512]{1,0:T(8,128)(2,1)} %param.4) | copy-start | bytes 1966084
  441.5 9.7 %all-to-all-start.3 = ((f32[1,5,16,640]{3,0,1,2:T(1,128)}), f32[1,5,16,640]{3,0,1,2:T(1,128)S(1)}, u32[]{:S(2)}, u32[]{:S(2)}) async-start(f32[1,5,16,640]{3,0,1,2:T(1,128)} %copy.286), calls=%async_computation.3 | async-start | bytes 409600 | tf_op jit(solution)/shard_map/all_to_all | solution.py:180
  451.3 1.7 copy-start.3
Sparse Core Ops, SparseCore 0:
  150.2 35.9 all-gather.5
  190.0 17.0 all-gather.7

commit v5 on v3

--- a/solution.py
+++ b/solution.py
@@ -62,9 +62,16 @@
     return x[:, 0, :].T
 
 
+def gather_a2a(value, name):
+    n = lax.axis_size(name)
+    copies = jnp.broadcast_to(value[None], (n,) + value.shape)
+    return lax.all_to_all(copies, name, 0, 0, tiled=True)
+
+
 def psum_tree(value):
-    for name in ("c", "z", "x"):
-        value = lax.psum(value, name)
+    value = lax.psum(value, "c")
+    for name in ("z", "x"):
+        value = jnp.sum(gather_a2a(value, name), axis=0)
     return value
 
 
@@ -130,8 +137,9 @@
         return (scale[:, None] * beta).astype(jnp.bfloat16)
 
     owned = lax.map(solve_own, jnp.arange(per_device, dtype=jnp.int32))
-    collected = lax.all_gather(owned, "z", axis=0, tiled=True)
-    collected = lax.all_gather(collected, "x", axis=0, tiled=True)
+    collected = gather_a2a(owned, "z")
+    collected = gather_a2a(collected.reshape((-1,) + owned.shape[1:]), "x")
+    collected = collected.reshape((-1,) + owned.shape[1:])
     coef = collected[:systems_count].reshape(FOLDS, SHRINK, width, traits_count)
     coef_flat = coef.transpose(2, 0, 1, 3).reshape(width, FOLDS * SHRINK * traits_count)
     shift = jnp.einsum("v,klvt->klt", mean, coef.astype(jnp.float32), precision=HIGH)

time: 511 us -> 481 us (0.941)
  blocking collectives: 89.6 us -> 29.1 us
  waiting for transfers between devices: 206 us -> 229 us
  starting transfers between devices: 4.86 us -> 11.8 us
    psum x3 -> x1, blocking collectives: 52.2 us -> 3.52 us  [psum_tree(): value = lax.psum(value, 'c')]
    all_gather x2 -> x0, blocking collectives: 37.4 us -> none  [the longest x1 24.6 us: shards(): collected = lax.all_gather(owned, 'z', axis=0, tiled=True)]
    all_to_all x0 -> x2, blocking collectives: none -> 25.6 us  [gather_a2a(): return lax.all_to_all(copies, name, 0, 0, tiled=True)]
    all_to_all x0 -> x2, waiting for transfers between devices: none -> 20.6 us  [gather_a2a(): return lax.all_to_all(copies, name, 0, 0, tiled=True)]
    all_to_all x0 -> x2, starting transfers between devices: none -> 6.99 us  [gather_a2a(): return lax.all_to_all(copies, name, 0, 0, tiled=True)]
  transfers between devices with their start and end apart: 2 -> 4, of which waited for: 2 -> 4; matrix products, arithmetic and copies ran while one was open for 0% -> 0% of each run, Pallas kernels for 0% -> 0%
where the time goes in v5:
time: 481 us; the launch traced here: 476 us
  waiting for transfers between devices  229 us (48%)
  other arithmetic  142 us (30%)
  blocking collectives  29.1 us (6%)
  local copies, waits for them, and re-layouts  26.3 us (5%)
  between operations  19.2 us (4%)
  matrix products  15.8 us (3%)
  starting transfers between devices  11.8 us (2%)
    psum x1, waiting for transfers between devices, shards(): stats = lax.psum(stats, SAMP)  204 us
    another operation x14, other arithmetic, solve_batch(): factors = jnp.linalg.cholesky(systems)  79 us
    another operation x3, other arithmetic, solve_single(): return jax.scipy.linalg.cho_solve((factor, True), right_side)  39.4 us
    all_to_all x2, blocking collectives, gather_a2a(): return lax.all_to_all(copies, name, 0, 0, tiled=True)  25.6 us
    all_to_all x2, waiting for transfers between devices, gather_a2a(): return lax.all_to_all(copies, name, 0, 0, tiled=True)  20.6 us
  transfers between devices with their start and end apart: 4, of which 4 were waited for; matrix products, arithmetic and copies ran while one was open for 0% of the time, Pallas kernels for 0%

profile of v5, /device:TPU:8, one launch (start us, length us, event | category | flops | bytes accessed | tf_op | source)
XLA Modules:
  0.0 475.8 jit_solution(6493887037403398760)
XLA Ops:
  7.2 1.4 copy.318
  8.6 1.3 convert_bitcast_fusion
  9.9 0.9 pad_maximum_fusion
  10.8 5.5 %fusion.2 = f32[5,529,529]{1,2,0:T(8,128)} fusion(bf16[640,529]{0,1:T(8,128)(2,1)S(1)} %pad_maximum_fusion, bf16[5,640]{1,0:T(8,128)(2,1)S(1)} %get-tuple-element.148), kind=kOutput, calls=%fused_computation.7 | convolution fusion | flops 1792675200 | bytes 6280340 | tf_op jit(solution)/shard_map/ri,krj->kij/dot_general | solution.py:89
  17.6 203.8 %all-reduce.3.cloned.1.call-done = f32[5,529,529]{1,2,0:T(8,128)} async-done(((f32[5,529,529]{1,2,0:T(8,128)}), f32[5,529,529]{1,2,0:T(8,128)}) %all-reduce.3.cloned.1.call-update) | async-done | bytes 5596836 | tf_op jit(solution)/shard_map/psum | solution.py:90
  221.4 1.5 slice_reduce_fusion.1
  223.4 0.9 fusion.101
  225.5 6.1 %fusion.102 = (f32[5,512,512]{1,2,0:T(8,128)}, f32[512,512]{0,1:T(8,128)S(1)}) fusion(f32[5,529,529]{1,2,0:T(8,128)} %all-reduce.3.cloned.1.call-done), kind=kLoop, calls=%fused_computation.212 | loop fusion | flops 1048576 | bytes 11534336 | tf_op jit(solution)/shard_map/slice | solution.py:91
  231.6 4.7 gather_fusion
  237.5 2.4 fusion.35
  240.5 11.7 %custom-call.46 = f32[1,128,128]{2,1,0:T(8,128)S(1)} custom-call(f32[1,128,128]{2,1,0:T(8,128)S(1)} %cholesky.264), custom_call_target="Cholesky" | custom-call | tf_op jit(solution)/shard_map/while/body/eval_jaxpr/jit(cholesky)/cholesky | solution.py:20
  252.3 9.8 %custom-call.47 = f32[1,1,128,128]{2,3,1,0:T(8,128)S(1)} custom-call(f32[1,1,128,128]{3,2,1,0:T(8,128)S(1)} %get-tuple-element.143), custom_call_target="InvertDiagBlocksLowerTriangular" | custom-call | tf_op jit(solution)/shard_map/while/body/eval_jaxpr/jit(cholesky)/cholesky | solution.py:20
  263.0 11.7 %custom-call.48 = f32[1,128,128]{2,1,0:T(8,128)S(1)} custom-call(f32[1,128,128]{2,1,0:T(8,128)S(1)} %cholesky.268), custom_call_target="Cholesky" | custom-call | tf_op jit(solution)/shard_map/while/body/eval_jaxpr/jit(cholesky)/cholesky | solution.py:20
  275.0 10.0 %custom-call.49 = f32[1,1,128,128]{2,3,1,0:T(8,128)S(1)} custom-call(f32[1,1,128,128]{3,2,1,0:T(8,128)S(1)} %get-tuple-element.141), custom_call_target="InvertDiagBlocksLowerTriangular" | custom-call | tf_op jit(solution)/shard_map/while/body/eval_jaxpr/jit(cholesky)/cholesky | solution.py:20
  285.9 11.7 %custom-call.50 = f32[1,128,128]{2,1,0:T(8,128)S(1)} custom-call(f32[1,128,128]{2,1,0:T(8,128)S(1)} %cholesky.273), custom_call_target="Cholesky" | custom-call | tf_op jit(solution)/shard_map/while/body/eval_jaxpr/jit(cholesky)/cholesky | solution.py:20
  297.8 9.8 %custom-call.51 = f32[1,1,128,128]{2,3,1,0:T(8,128)S(1)} custom-call(f32[1,1,128,128]{3,2,1,0:T(8,128)S(1)} %get-tuple-element.139), custom_call_target="InvertDiagBlocksLowerTriangular" | custom-call | tf_op jit(solution)/shard_map/while/body/eval_jaxpr/jit(cholesky)/cholesky | solution.py:20
  308.4 12.1 %custom-call.52 = f32[1,128,128]{2,1,0:T(8,128)S(1)} custom-call(f32[1,128,128]{2,1,0:T(8,128)S(1)} %fusion.21), custom_call_target="Cholesky" | custom-call | tf_op jit(solution)/shard_map/while/body/eval_jaxpr/jit(cholesky)/cholesky | solution.py:20
  321.9 0.7 compare_reduce_fusion.2
  325.3 8.1 %while.1 = (s32[]{:T(128)}, f32[1,512,512]{1,2,0:T(8,128)S(1)}, s32[4,2]{0,1:T(2,128)S(1)}, f32[4,1,128,128]{3,2,1,0:T(8,128)S(1)}, s32[]{:T(128)}) while((s32[]{:T(128)}, f32[1,512,512]{1,2,0:T(8,128)S(1)}, s32[4,2]{0,1:T(2,128)S(1)}, f32[4,1,128,128]{3,2,1,0:T(8,128)S(1)}, s32[]{:T(128)}) %tuple.60), condition=%wide.while_cond, body=%wide.while_body.sunk | while | flops 2 | bytes 393333 | solution.py:23
  325.9 1.3 constant_dynamic-slice_fusion.11
  328.0 1.3 constant_dynamic-slice_fusion.11
  330.0 1.3 constant_dynamic-slice_fusion.11
  332.0 1.3 constant_dynamic-slice_fusion.11
  333.5 39.3 %custom-call.53 = f32[1,4,128,128]{2,3,1,0:T(8,128)S(1)} custom-call(f32[1,4,128,128]{3,2,1,0:T(8,128)S(1)} %bitcast.363), custom_call_target="InvertDiagBlocksLowerTriangular" | custom-call | tf_op jit(solution)/shard_map/while/body/eval_jaxpr/vmap(jit(_cho_solve))/triangular_solve | solution.py:23
  372.8 1.8 fusion.100
  374.6 0.7 copy.329
  375.4 0.8 fusion.99
  376.3 0.8 fusion.66
  380.1 14.7 %all_to_all.35 = bf16[8,1,512,16]{2,3,1,0:T(8,128)(2,1)S(1)} all-to-all(bf16[8,1,512,16]{2,3,1,0:T(8,128)(2,1)S(1)} %broadcast_in_dim.63), channel_id=1, replica_groups=mesh['x'=4,'z'=8,'c'=2,'blk'=4] {'z'}, dimensions={0} | all-to-all | bytes 262144 | tf_op jit(solution)/shard_map/all_to_all | solution.py:68
  394.9 10.9 %all_to_all.36 = bf16[4,8,512,16]{2,3,1,0:T(8,128)(2,1)S(1)} all-to-all(bf16[4,8,512,16]{2,3,1,0:T(8,128)(2,1)S(1)} %broadcast_in_dim.67), channel_id=1, replica_groups=mesh['x'=4,'z'=8,'c'=2,'blk'=4] {'x'}, dimensions={0} | all-to-all | bytes 1048576 | tf_op jit(solution)/shard_map/all_to_all | solution.py:68
  405.8 1.5 fusion.104
  407.8 0.9 copy.330
  408.7 4.8 %all-to-all-start.2 = ((f32[1,5,16,640]{3,0,1,2:T(1,128)}), f32[1,5,16,640]{3,0,1,2:T(1,128)S(1)}, u32[]{:S(2)}, u32[]{:S(2)}) async-start(f32[1,5,16,640]{3,0,1,2:T(1,128)} %copy.330), calls=%async_computation.2 | async-start | bytes 409600 | tf_op jit(solution)/shard_map/all_to_all | solution.py:153
  413.5 0.7 dynamic-slice_convert_fusion
  414.2 4.2 all-to-all-done.2
  419.7 1.4 fusion.13
  421.3 3.5 psum.15
  424.8 0.8 broadcast_in_dim.69
  425.6 3.5 all-to-all-start.3
  430.2 14.2 %all-to-all-done.3 = f32[8,20,440]{2,1,0:T(8,128)S(1)} async-done(((f32[8,20,440]{2,1,0:T(8,128)}), f32[8,20,440]{2,1,0:T(8,128)S(1)}, u32[]{:S(2)}, u32[]{:S(2)}) %all-to-all-start.3) | async-done | bytes 281632 | tf_op jit(solution)/shard_map/all_to_all | solution.py:68
  444.5 0.7 broadcast_in_dim.70
  445.2 3.5 all-to-all-start.4
  448.7 6.4 %all-to-all-done.4 = f32[4,20,440]{2,1,0:T(8,128)S(1)} async-done(((f32[4,20,440]{2,1,0:T(8,128)}), f32[4,20,440]{2,1,0:T(8,128)S(1)}, u32[]{:S(2)}, u32[]{:S(2)}) %all-to-all-start.4) | async-done | bytes 140832 | tf_op jit(solution)/shard_map/all_to_all | solution.py:68
  455.9 0.8 gather_fusion.1
  461.3 0.8 add_bitcast_fusion.a_ref
  462.1 2.4 shard_map.59
  464.5 0.8 copy.413
  465.6 0.7 copy.368
  (163 shorter events, 24.6 us)
Async XLA Ops:
  7.2 214.3 %all-reduce.3.cloned.1.call-start = ((), (), s32[]{:S(2)}) async-start(), calls=%async_computation.5 | async-start | bytes 13721600 | tf_op jit(solution)/shard_map/psum | solution.py:90
  16.3 0.7 copy-start.4
  374.6 32.7 %copy-start = (bf16[640,512]{1,0:T(8,128)(2,1)S(1)}, bf16[640,512]{1,0:T(8,128)(2,1)}, u32[]{:S(2)}) copy-start(bf16[640,512]{1,0:T(8,128)(2,1)} %param.4) | copy-start | bytes 1966084
  375.3 32.0 %copy-start.1 = (f32[640,5]{0,1:T(8,128)S(1)}, f32[640,5]{0,1:T(8,128)}, u32[]{:S(2)}) copy-start(f32[640,5]{0,1:T(8,128)} %get-tuple-element.147) | copy-start | bytes 38404
  394.9 23.8 %copy-start.2 = (s32[640]{0:T(1024)S(1)}, s32[640]{0:T(1024)}, u32[]{:S(2)}) copy-start(s32[640]{0:T(1024)} %param.6) | copy-start | bytes 7684
  405.8 13.9 %copy-start.3 = (f32[640,5]{0,1:T(8,128)S(1)}, f32[640,5]{0,1:T(8,128)}, u32[]{:S(2)}) copy-start(f32[640,5]{0,1:T(8,128)} %get-tuple-element.146) | copy-start | bytes 38404
  408.7 9.7 %all-to-all-start.2 = ((f32[1,5,16,640]{3,0,1,2:T(1,128)}), f32[1,5,16,640]{3,0,1,2:T(1,128)S(1)}, u32[]{:S(2)}, u32[]{:S(2)}) async-start(f32[1,5,16,640]{3,0,1,2:T(1,128)} %copy.330), calls=%async_computation.2 | async-start | bytes 409600 | tf_op jit(solution)/shard_map/all_to_all | solution.py:153
  425.6 18.8 %all-to-all-start.3 = ((f32[8,20,440]{2,1,0:T(8,128)}), f32[8,20,440]{2,1,0:T(8,128)S(1)}, u32[]{:S(2)}, u32[]{:S(2)}) async-start(f32[8,20,440]{2,1,0:T(8,128)} %broadcast_in_dim.69), calls=%async_computation.3 | async-start | bytes 786432 | tf_op jit(solution)/shard_map/all_to_all | solution.py:68
  445.2 10.0 %all-to-all-start.4 = ((f32[4,20,440]{2,1,0:T(8,128)}), f32[4,20,440]{2,1,0:T(8,128)S(1)}, u32[]{:S(2)}, u32[]{:S(2)}) async-start(f32[4,20,440]{2,1,0:T(8,128)} %broadcast_in_dim.70), calls=%async_computation.4 | async-start | bytes 393216 | tf_op jit(solution)/shard_map/all_to_all | solution.py:68
Sparse Core Ops, SparseCore 0:
  16.5 204.8 all-reduce.2

commit v6 on v5

--- a/solution.py
+++ b/solution.py
@@ -23,6 +23,41 @@
         return jax.scipy.linalg.cho_solve((factor, True), right_side)
 
     return jax.vmap(solve_single)(factors, right_sides)
+
+
+def blocked_cholesky_solve(system, target, block=128):
+    size = system.shape[0]
+    count = size // block
+    eye = jnp.eye(block, dtype=system.dtype)
+    tiles = {
+        (i, j): system[i * block : (i + 1) * block, j * block : (j + 1) * block]
+        for i in range(count)
+        for j in range(i + 1)
+    }
+    factors, inverses = {}, {}
+    for j in range(count):
+        diagonal = jnp.linalg.cholesky(tiles[j, j])
+        inverse = jax.scipy.linalg.solve_triangular(diagonal, eye, lower=True)
+        inverses[j] = inverse
+        for i in range(j + 1, count):
+            factors[i, j] = jnp.dot(tiles[i, j], inverse.T, precision=HIGH)
+        for i in range(j + 1, count):
+            for k in range(j + 1, i + 1):
+                tiles[i, k] = tiles[i, k] - jnp.dot(factors[i, j], factors[k, j].T, precision=HIGH)
+    parts = [target[j * block : (j + 1) * block] for j in range(count)]
+    solved = []
+    for j in range(count):
+        rest = parts[j]
+        for p in range(j):
+            rest = rest - jnp.dot(factors[j, p], solved[p], precision=HIGH)
+        solved.append(jnp.dot(inverses[j], rest, precision=HIGH))
+    result = [None] * count
+    for j in reversed(range(count)):
+        rest = solved[j]
+        for i in range(j + 1, count):
+            rest = rest - jnp.dot(factors[i, j].T, result[i], precision=HIGH)
+        result[j] = jnp.dot(inverses[j].T, rest, precision=HIGH)
+    return jnp.concatenate(result, axis=0)
 
 
 def _cholesky_solve_kernel(a_ref, b_ref, x_ref):
@@ -133,7 +168,7 @@
         penalty = jnp.sum(
             jnp.where(jnp.arange(SHRINK, dtype=jnp.int32) == shrink, ratios * width, 0.0)
         )
-        beta = solve_batch((system + penalty * identity)[None], target[None])[0]
+        beta = blocked_cholesky_solve(system + penalty * identity, target)
         return (scale[:, None] * beta).astype(jnp.bfloat16)
 
     owned = lax.map(solve_own, jnp.arange(per_device, dtype=jnp.int32))

time: 481 us -> 445 us (0.925)
  other arithmetic: 142 us -> 114 us
  local copies, waits for them, and re-layouts: 26.3 us -> 17.1 us
    another operation x19 -> x22, other arithmetic: 120 us -> 93.4 us  [the longest x12 50.1 us: blocked_cholesky_solve(): diagonal = jnp.linalg.cholesky(tiles[j, j])]
    another operation x34 -> x0, local copies, waits for them, and re-layouts: 8.66 us -> none
    dot_general x0 -> x36, matrix products: none -> 8.27 us  [the longest x10 2.67 us: blocked_cholesky_solve(): jnp.dot(factors[i, j], factors[k, j].T, precision=HIGH)]
where the time goes in v6:
time: 445 us; the launch traced here: 440 us
  waiting for transfers between devices  229 us (51%)
  other arithmetic  114 us (26%)
  blocking collectives  29.1 us (7%)
  matrix products  20 us (4%)
  local copies, waits for them, and re-layouts  17.1 us (4%)
  between operations  16.8 us (4%)
  starting transfers between devices  11.8 us (3%)
    psum x1, waiting for transfers between devices, shards(): stats = lax.psum(stats, SAMP)  204 us
    another operation x12, other arithmetic, blocked_cholesky_solve(): diagonal = jnp.linalg.cholesky(tiles[j, j])  50.1 us
    another operation x8, other arithmetic, blocked_cholesky_solve(): inverse = jax.scipy.linalg.solve_triangular(diagonal, eye, lower=True)  41.9 us
    all_to_all x2, blocking collectives, gather_a2a(): return lax.all_to_all(copies, name, 0, 0, tiled=True)  25.6 us
    all_to_all x2, waiting for transfers between devices, gather_a2a(): return lax.all_to_all(copies, name, 0, 0, tiled=True)  20.6 us
  transfers between devices with their start and end apart: 4, of which 4 were waited for; matrix products, arithmetic and copies ran while one was open for 0% of the time, Pallas kernels for 0%

profile of v6, /device:TPU:8, one launch (start us, length us, event | category | flops | bytes accessed | tf_op | source)
XLA Modules:
  0.0 440.2 jit_solution(6431359175789549743)
XLA Ops:
  7.2 1.4 copy.345
  8.6 0.7 convert_bitcast_fusion
  9.3 0.9 pad_maximum_fusion
  10.2 5.5 %fusion.2 = f32[5,529,529]{1,2,0:T(8,128)} fusion(bf16[640,529]{0,1:T(8,128)(2,1)S(1)} %pad_maximum_fusion, bf16[5,640]{1,0:T(8,128)(2,1)S(1)} %get-tuple-element.94), kind=kOutput, calls=%fused_computation.4 | convolution fusion | flops 1792675200 | bytes 6280340 | tf_op jit(solution)/shard_map/ri,krj->kij/dot_general | solution.py:124
  17.0 203.9 %all-reduce.2.cloned.1.call-done = f32[5,529,529]{1,2,0:T(8,128)} async-done(((f32[5,529,529]{1,2,0:T(8,128)}), f32[5,529,529]{1,2,0:T(8,128)}) %all-reduce.2.cloned.1.call-update) | async-done | bytes 5596836 | tf_op jit(solution)/shard_map/psum | solution.py:125
  220.9 1.5 slice_reduce_fusion.1
  222.9 0.9 fusion.89
  225.0 6.1 %fusion.90 = (f32[5,512,512]{1,2,0:T(8,128)}, f32[512,512]{0,1:T(8,128)S(1)}) fusion(f32[5,529,529]{1,2,0:T(8,128)} %all-reduce.2.cloned.1.call-done), kind=kLoop, calls=%fused_computation.180 | loop fusion | flops 1048576 | bytes 11534336 | tf_op jit(solution)/shard_map/slice | solution.py:126
  231.1 4.7 %gather_fusion = f32[512]{0:T(512)S(1)} fusion(f32[512,512]{0,1:T(8,128)S(1)} %get-tuple-element.89, s32[512]{0:T(512)S(1)} %bitcast.257), kind=kCustom, calls=%fused_computation | custom fusion | bytes 8192 | tf_op jit(solution)/shard_map/jit(diagonal)/cond/branch_0_fun/gather | solution.py:134
  237.1 2.3 fusion.23
  239.6 11.7 %cholesky.74 = f32[128,128]{1,0:T(8,128)S(1)} custom-call(f32[128,128]{1,0:T(8,128)S(1)} %fusion.67), custom_call_target="Cholesky" | custom-call | tf_op jit(solution)/shard_map/while/body/eval_jaxpr/jit(cholesky)/cholesky | solution.py:39
  252.0 0.7 fusion.50
  252.6 9.8 %custom-call.12 = f32[1,128,128]{1,2,0:T(8,128)S(1)} custom-call(f32[1,128,128]{2,1,0:T(8,128)S(1)} %fusion.50), custom_call_target="InvertDiagBlocksLowerTriangular" | custom-call | tf_op jit(solution)/shard_map/while/body/eval_jaxpr/jit(_solve_triangular)/triangular_solve | solution.py:40
  265.2 1.8 fusion.88
  267.2 0.8 fusion.87
  269.2 11.9 %cholesky.85 = f32[128,128]{1,0:T(8,128)S(1)} custom-call(f32[128,128]{1,0:T(8,128)S(1)} %fusion.65), custom_call_target="Cholesky" | custom-call | tf_op jit(solution)/shard_map/while/body/eval_jaxpr/jit(cholesky)/cholesky | solution.py:39
  281.1 0.6 compare_reduce_fusion.2
  281.8 0.7 fusion.51
  282.4 9.8 %custom-call.13 = f32[1,128,128]{1,2,0:T(8,128)S(1)} custom-call(f32[1,128,128]{2,1,0:T(8,128)S(1)} %fusion.51), custom_call_target="InvertDiagBlocksLowerTriangular" | custom-call | tf_op jit(solution)/shard_map/while/body/eval_jaxpr/jit(_solve_triangular)/triangular_solve | solution.py:40
  294.0 11.7 %cholesky.96 = f32[128,128]{1,0:T(8,128)S(1)} custom-call(f32[128,128]{1,0:T(8,128)S(1)} %fusion.63), custom_call_target="Cholesky" | custom-call | tf_op jit(solution)/shard_map/while/body/eval_jaxpr/jit(cholesky)/cholesky | solution.py:39
  305.8 0.6 compare_reduce_fusion.1
  306.4 0.7 fusion.52
  307.1 9.8 %custom-call.14 = f32[1,128,128]{1,2,0:T(8,128)S(1)} custom-call(f32[1,128,128]{2,1,0:T(8,128)S(1)} %fusion.52), custom_call_target="InvertDiagBlocksLowerTriangular" | custom-call | tf_op jit(solution)/shard_map/while/body/eval_jaxpr/jit(_solve_triangular)/triangular_solve | solution.py:40
  317.9 12.1 %cholesky.107 = f32[128,128]{1,0:T(8,128)S(1)} custom-call(f32[128,128]{1,0:T(8,128)S(1)} %fusion.61), custom_call_target="Cholesky" | custom-call | tf_op jit(solution)/shard_map/while/body/eval_jaxpr/jit(cholesky)/cholesky | solution.py:39
  330.0 0.6 compare_reduce_fusion
  330.7 0.7 fusion.53
  331.3 9.8 %custom-call.15 = f32[1,128,128]{1,2,0:T(8,128)S(1)} custom-call(f32[1,128,128]{2,1,0:T(8,128)S(1)} %fusion.53), custom_call_target="InvertDiagBlocksLowerTriangular" | custom-call | tf_op jit(solution)/shard_map/while/body/eval_jaxpr/jit(_solve_triangular)/triangular_solve | solution.py:40
  344.5 14.7 %all_to_all.35 = bf16[8,1,512,16]{2,3,1,0:T(8,128)(2,1)S(1)} all-to-all(bf16[8,1,512,16]{2,3,1,0:T(8,128)(2,1)S(1)} %broadcast_in_dim.52), channel_id=1, replica_groups=mesh['x'=4,'z'=8,'c'=2,'blk'=4] {'z'}, dimensions={0} | all-to-all | bytes 262144 | tf_op jit(solution)/shard_map/all_to_all | solution.py:103
  359.3 10.9 %all_to_all.36 = bf16[4,8,512,16]{2,3,1,0:T(8,128)(2,1)S(1)} all-to-all(bf16[4,8,512,16]{2,3,1,0:T(8,128)(2,1)S(1)} %broadcast_in_dim.54), channel_id=1, replica_groups=mesh['x'=4,'z'=8,'c'=2,'blk'=4] {'x'}, dimensions={0} | all-to-all | bytes 1048576 | tf_op jit(solution)/shard_map/all_to_all | solution.py:103
  370.2 1.5 fusion.102
  372.3 0.9 copy.362
  373.2 4.8 %all-to-all-start.2 = ((f32[1,5,16,640]{3,0,1,2:T(1,128)}), f32[1,5,16,640]{3,0,1,2:T(1,128)S(1)}, u32[]{:S(2)}, u32[]{:S(2)}) async-start(f32[1,5,16,640]{3,0,1,2:T(1,128)} %copy.362), calls=%async_computation.2 | async-start | bytes 409600 | tf_op jit(solution)/shard_map/all_to_all | solution.py:188
  378.0 0.7 dynamic-slice_convert_fusion
  378.7 4.2 all-to-all-done.2
  384.1 1.4 fusion.13
  385.7 3.5 psum.15
  389.2 0.8 broadcast_in_dim.56
  390.0 3.5 all-to-all-start.3
  394.6 14.2 %all-to-all-done.3 = f32[8,20,440]{2,1,0:T(8,128)S(1)} async-done(((f32[8,20,440]{2,1,0:T(8,128)}), f32[8,20,440]{2,1,0:T(8,128)S(1)}, u32[]{:S(2)}, u32[]{:S(2)}) %all-to-all-start.3) | async-done | bytes 281632 | tf_op jit(solution)/shard_map/all_to_all | solution.py:103
  408.9 0.7 broadcast_in_dim.57
  409.6 3.5 all-to-all-start.4
  413.1 6.4 %all-to-all-done.4 = f32[4,20,440]{2,1,0:T(8,128)S(1)} async-done(((f32[4,20,440]{2,1,0:T(8,128)}), f32[4,20,440]{2,1,0:T(8,128)S(1)}, u32[]{:S(2)}, u32[]{:S(2)}) %all-to-all-start.4) | async-done | bytes 140832 | tf_op jit(solution)/shard_map/all_to_all | solution.py:103
  420.4 0.8 gather_fusion.1
  425.7 0.8 add_bitcast_fusion.a_ref
  426.5 2.4 shard_map.59
  428.9 0.8 copy.452
  430.1 0.7 copy.400
  432.5 0.7 multiply_bitcast_fusion.1
  (153 shorter events, 24.0 us)
Async XLA Ops:
  7.2 213.7 %all-reduce.2.cloned.1.call-start = ((), (), s32[]{:S(2)}) async-start(), calls=%async_computation.5 | async-start | bytes 13721600 | tf_op jit(solution)/shard_map/psum | solution.py:125
  15.7 0.7 copy-start.2
  293.7 78.1 %copy-start = (bf16[640,512]{1,0:T(8,128)(2,1)S(1)}, bf16[640,512]{1,0:T(8,128)(2,1)}, u32[]{:S(2)}) copy-start(bf16[640,512]{1,0:T(8,128)(2,1)} %param.7) | copy-start | bytes 1966084
  359.3 23.8 %copy-start.1 = (s32[640]{0:T(1024)S(1)}, s32[640]{0:T(1024)}, u32[]{:S(2)}) copy-start(s32[640]{0:T(1024)} %param.9) | copy-start | bytes 7684
  373.2 9.7 %all-to-all-start.2 = ((f32[1,5,16,640]{3,0,1,2:T(1,128)}), f32[1,5,16,640]{3,0,1,2:T(1,128)S(1)}, u32[]{:S(2)}, u32[]{:S(2)}) async-start(f32[1,5,16,640]{3,0,1,2:T(1,128)} %copy.362), calls=%async_computation.2 | async-start | bytes 409600 | tf_op jit(solution)/shard_map/all_to_all | solution.py:188
  390.0 18.8 %all-to-all-start.3 = ((f32[8,20,440]{2,1,0:T(8,128)}), f32[8,20,440]{2,1,0:T(8,128)S(1)}, u32[]{:S(2)}, u32[]{:S(2)}) async-start(f32[8,20,440]{2,1,0:T(8,128)} %broadcast_in_dim.56), calls=%async_computation.3 | async-start | bytes 786432 | tf_op jit(solution)/shard_map/all_to_all | solution.py:103
  409.6 10.0 %all-to-all-start.4 = ((f32[4,20,440]{2,1,0:T(8,128)}), f32[4,20,440]{2,1,0:T(8,128)S(1)}, u32[]{:S(2)}, u32[]{:S(2)}) async-start(f32[4,20,440]{2,1,0:T(8,128)} %broadcast_in_dim.57), calls=%async_computation.4 | async-start | bytes 393216 | tf_op jit(solution)/shard_map/all_to_all | solution.py:103
Sparse Core Ops, SparseCore 0:
  15.9 204.9 all-reduce.1
